TPU v7x, 32 devices: a whole 2x2x4 slice. The times are simulated.
32 devices in a mesh: sta: 4 (over y, x), evt: 8 (over z, core).
Axes of the slice: x: 2, y: 2, z: 4, core: 2. Of those that a mesh axis runs over, the one named last changes fastest.
Arguments:
- traces: bfloat16 [512, 96, 280], P('evt', 'sta'), may hold values from -400 to 400, as said below
- channel_valid: int32 [96], P('sta'), may hold values 0 or 1
- partner_block: int32 [512, 2], P('evt'), may hold values from 0 to 7, all different within a row; in each aligned block of 64 rows (0 to 63, 64 to 127, ...) at most 16 rows name the same one
Outputs:
- coefficient: float32 [512, 81, 128], P('evt')
Inputs may be any that keep to these rules, and one draw needn't show every extreme that they name: `partner_block`: each event names 2 different blocks; among the 64 events of one block no block is named more than 16 times, and some block is named exactly 16 times. `traces`: finite trace samples.
All inputs are finite; a program needn't handle non-finite values. No bound on the sum of `channel_valid` on one device may be relied on, other than what follows from the above.
Results may differ from a plain program's by a relative error of at most 0.0003.
Values may be sent and summed in bfloat16 or wider, within the bound.
No kernel may reach another device: no remote copies, remote signals or barrier semaphores. Data moves between devices by JAX's collectives and lax.ppermute only.
A program may use at most 64 MiB of HBM per device.

v0:
```python
import jax
import jax.numpy as jnp
from jax import lax
from jax.experimental.layout import Layout, with_layout_constraint
from jax.sharding import PartitionSpec as P

WIN = 200
MAXLAG = 40
FOLD = 4


def band_table(extent, lag_count):
    sample = jnp.arange(extent, dtype=jnp.int32)[:, None]
    shift = jnp.arange(lag_count, dtype=jnp.int32)[None, :]
    return ((sample >= shift) & (sample < shift + WIN)).astype(jnp.float32)


def normalize(lag_scores, slot_energy, event_energy):
    return lag_scores / jnp.sqrt(event_energy[:, None, None] * slot_energy[None, :, :] + 1e-06)


def exchange(value, axis, bit, size):
    return lax.ppermute(value, axis, [(i, i ^ bit) for i in range(size)])


def pick(pair, upper):
    return jnp.where(upper, pair[1], pair[0]), jnp.where(upper, pair[0], pair[1])


def place(mine, other, upper):
    return jnp.where(upper, jnp.stack([other, mine]), jnp.stack([mine, other]))


def sta_allreduce(data):
    axis = "sta"
    size = lax.axis_size(axis)
    if size & (size - 1) or size == 1:
        return lax.psum(data, axis)
    index = lax.axis_index(axis)
    bits = [1 << k for k in range(size.bit_length() - 1)]
    orders = [bits, bits[::-1]]
    half = data.shape[0] // 2
    accs = [data[:half], data[half:]]
    for stage in range(len(bits)):
        sends, keeps = [], []
        for h in range(2):
            bit = orders[h][stage]
            acc = accs[h].reshape((2, accs[h].shape[0] // 2) + accs[h].shape[1:])
            keep, send = pick(acc, (index & bit) != 0)
            sends.append(send)
            keeps.append(keep)
        sends = lax.optimization_barrier(sends)
        got = [exchange(sends[h], axis, orders[h][stage], size) for h in range(2)]
        got = lax.optimization_barrier(got)
        accs = [keeps[h] + got[h] for h in range(2)]
    for stage in reversed(range(len(bits))):
        accs = lax.optimization_barrier(accs)
        got = [exchange(accs[h], axis, orders[h][stage], size) for h in range(2)]
        got = lax.optimization_barrier(got)
        accs = [
            place(accs[h], got[h], (index & orders[h][stage]) != 0).reshape(
                (-1,) + accs[h].shape[1:]
            )
            for h in range(2)
        ]
    return jnp.concatenate(accs, axis=0)


def body(traces, channel_valid, partner_block):
    events, channels, extent = traces.shape
    partners = partner_block.shape[1]
    devices_evt = lax.axis_size("evt")
    sta_size = lax.axis_size("sta")
    capacity = max(2, (events * partners + devices_evt - 1) // devices_evt)
    slot_count = devices_evt * capacity
    lag_count = extent - WIN + 1
    flat = partner_block.reshape(-1)
    owner_hot = (flat[:, None] == jnp.arange(devices_evt, dtype=jnp.int32)[None, :]).astype(
        jnp.int32
    )
    before = jnp.cumsum(owner_hot, axis=0) - owner_hot
    ranking = jnp.sum(before * owner_hot, axis=1)
    target = flat * capacity + ranking
    slot_hot = (target[:, None] == jnp.arange(slot_count, dtype=jnp.int32)[None, :]).astype(
        jnp.bfloat16
    )
    row_event = jnp.arange(events * partners, dtype=jnp.int32) // partners
    event_hot = (row_event[:, None] == jnp.arange(events, dtype=jnp.int32)[None, :]).astype(
        jnp.bfloat16
    )
    selection = jnp.dot(slot_hot.T, event_hot, preferred_element_type=jnp.float32).astype(
        jnp.bfloat16
    )
    outgoing = jnp.dot(
        selection, traces.reshape(events, channels * extent), preferred_element_type=jnp.float32
    ).astype(jnp.bfloat16)
    received = lax.all_to_all(
        outgoing.reshape(slot_count, channels, extent),
        "evt",
        split_axis=0,
        concat_axis=0,
        tiled=True,
    )
    valid = channel_valid.astype(jnp.bfloat16)
    template = traces[:, :, MAXLAG : MAXLAG + WIN] * valid[None, :, None]
    fold = FOLD
    positions = -(-lag_count // fold)
    span = WIN + fold - 1
    reach = (positions - 1) * fold + span
    shifted = [
        jnp.pad(template, ((0, 0), (0, 0), (d, fold - 1 - d))) for d in range(fold)
    ]
    expanded = jnp.stack(shifted, axis=1).reshape(events * fold, channels, span)
    widened = jnp.pad(received, ((0, 0), (0, 0), (0, max(0, reach - extent))))
    lag_scores = lax.conv_general_dilated(
        widened,
        expanded,
        (fold,),
        "VALID",
        dimension_numbers=("NCH", "OIH", "CHN"),
        preferred_element_type=jnp.float32,
    )
    lag_scores = with_layout_constraint(lag_scores, Layout((0, 1, 2)))
    event_energy = jnp.sum(jnp.square(template.astype(jnp.float32)), axis=(1, 2))
    squares_sum = jnp.sum(
        jnp.square(received.astype(jnp.float32)) * channel_valid.astype(jnp.float32)[None, :, None],
        axis=1,
    )
    slot_energy = lax.dot_general(
        band_table(extent, lag_count),
        squares_sum,
        (((0,), (1,)), ((), ())),
        precision=lax.Precision.HIGHEST,
    )
    cells = positions * slot_count
    slot_rows = -(-slot_energy.size // cells)
    energy_rows = -(-events // cells)
    used = events * fold + slot_rows + energy_rows
    spare = -used % (4 * sta_size)
    flat_slot = jnp.pad(slot_energy.reshape(-1), (0, slot_rows * cells - slot_energy.size))
    flat_event = jnp.pad(event_energy, (0, energy_rows * cells - events))
    packed = jnp.concatenate(
        [
            lag_scores,
            flat_slot.reshape(slot_rows, positions, slot_count),
            flat_event.reshape(energy_rows, positions, slot_count),
            jnp.zeros((spare, positions, slot_count), jnp.float32),
        ],
        axis=0,
    )
    total = sta_allreduce(packed)
    base = events * fold
    slot_all = total[base : base + slot_rows].reshape(-1)[: lag_count * slot_count]
    event_all = total[base + slot_rows : base + slot_rows + energy_rows].reshape(-1)[:events]
    scores_all = total[:base].reshape(events, fold, positions, slot_count)
    scores_all = jnp.transpose(scores_all, (0, 2, 1, 3)).reshape(
        events, positions * fold, slot_count
    )[:, :lag_count]
    return normalize(scores_all, slot_all.reshape(lag_count, slot_count), event_all)


def solution(mesh):
    return jax.shard_map(
        body,
        mesh=mesh,
        in_specs=(P("evt", "sta", None), P("sta"), P("evt", None)),
        out_specs=P("evt", None, None),
        check_vma=False,
    )
```

profile of v0, /device:TPU:0, one launch (start us, length us, event | category | flops | bytes accessed | tf_op | source)
XLA Modules:
  0.0 155.1 jit_solution(11591843538200636605)
XLA Ops:
  0.0 0.8 copy.61
  0.8 0.1 reshape.104
  0.9 0.1 fusion.4
  1.0 0.2 reduce_window_sum.11
  1.2 0.2 select_reduce_fusion
  1.4 2.1 %reshape.105 = bf16[64,6720]{1,0:T(8,128)(2,1)S(1)} reshape(bf16[64,24,280]{2,1,0:T(8,128)(2,1)} %param.3) | data formatting | bytes 1720320 | tf_op jit(solution)/shard_map/reshape | solution.py:95
  3.5 0.9 convolution_convert_fusion
  4.4 2.9 %copy.62 = bf16[128,24,280]{2,1,0:T(8,128)(2,1)} copy(bf16[128,24,280]{0,2,1:T(8,128)(2,1)S(1)} %bitcast.49) | data formatting | bytes 3440640 | tf_op jit(solution)/shard_map/reshape | solution.py:98
  7.3 0.0 copy-start.2
  7.3 0.0 copy-start
  7.3 6.5 %all-to-all-start = ((bf16[128,24,280]{2,1,0:T(8,128)(2,1)}), bf16[128,24,280]{2,1,0:T(8,128)(2,1)S(1)}, u32[]{:S(2)}, u32[]{:S(2)}) async-start(bf16[128,24,280]{2,1,0:T(8,128)(2,1)} %copy.62), calls=%async_computation | async-start | bytes 4718592 | tf_op jit(solution)/shard_map/all_to_all | solution.py:97
  13.8 0.0 copy-done.2
  13.8 0.0 copy-done
  13.8 1.0 multiply_reduce_fusion.1
  14.8 0.9 pad_bitcast_fusion.3
  15.7 0.8 pad_maximum_fusion
  16.5 2.1 %copy.63 = bf16[64,4,24,203]{3,2,1,0:T(8,128)(2,1)} copy(bf16[64,4,24,203]{3,2,0,1:T(8,128)(2,1)S(1)} %pad_maximum_fusion) | data formatting | bytes 4988928 | tf_op jit(solution)/shard_map/stack | solution.py:113
  18.6 5.2 %copy.65 = bf16[256,24,203]{0,1,2:T(8,128)(2,1)} copy(bf16[256,24,203]{2,1,0:T(8,128)(2,1)} %bitcast.42) | data formatting | bytes 4988928 | tf_op jit(solution)/shard_map/reshape | solution.py:113
  23.8 0.1 pad_slice_fusion
  23.9 44.5 %all-to-all-done = bf16[128,24,280]{2,1,0:T(8,128)(2,1)S(1)} async-done(((bf16[128,24,280]{2,1,0:T(8,128)(2,1)}), bf16[128,24,280]{2,1,0:T(8,128)(2,1)S(1)}, u32[]{:S(2)}, u32[]{:S(2)}) %all-to-all-start) | async-done | bytes 1720352 | tf_op jit(solution)/shard_map/all_to_all | solution.py:97
  68.4 2.6 %copy.67 = bf16[128,24,280]{0,2,1:T(8,128)(2,1)} copy(bf16[128,24,280]{2,1,0:T(8,128)(2,1)S(1)} %all-to-all-done) | data formatting | bytes 3440640 | tf_op jit(solution)/shard_map/all_to_all | solution.py:97
  71.1 1.9 %multiply_reduce_fusion = f32[128,280]{0,1:T(8,128)S(1)} fusion(bf16[128,24,280]{0,2,1:T(8,128)(2,1)} %copy.67, f32[24]{0:T(128)S(1)} %get-tuple-element.48), kind=kLoop, calls=%fused_computation.1 | loop fusion | flops 3404800 | bytes 1863776 | tf_op jit(solution)/shard_map/reduce_sum | solution.py:125
  73.0 0.3 convolution_bitcast_fusion
  73.4 3.0 %copy.64 = bf16[128,24,280]{0,1,2:T(8,128)(2,1)} copy(bf16[128,24,280]{2,1,0:T(8,128)(2,1)S(1)} %all-to-all-done) | data formatting | bytes 3440640 | tf_op jit(solution)/shard_map/all_to_all | solution.py:97
  76.3 10.3 %fusion.11 = f32[256,21,128]{2,0,1:T(8,128)S(1)} fusion(bf16[128,24,280]{0,1,2:T(8,128)(2,1)} %copy.64, bf16[256,24,203]{0,1,2:T(8,128)(2,1)} %copy.65), kind=kOutput, calls=%fused_computation.49 | convolution fusion | flops 6700400640 | bytes 6967296 | tf_op jit(solution)/shard_map/conv_general_dilated | solution.py:115
  86.6 1.6 %copy.66 = f32[256,21,128]{2,1,0:T(8,128)S(1)} copy(f32[256,21,128]{2,0,1:T(8,128)S(1)} %fusion.11) | data formatting | bytes 5505024 | tf_op jit(solution)/shard_map/conv_general_dilated | solution.py:115
  88.2 0.3 slice_select_fusion
  88.5 0.1 copy.69
  88.6 0.1 copy.70
  88.8 1.6 %collective-permute-start.1 = (f32[68,21,128]{2,0,1:T(8,128)S(1)}, f32[68,21,128]{2,0,1:T(8,128)S(1)}, u32[]{:S(2)}, u32[]{:S(2)}) collective-permute-start(f32[68,21,128]{2,0,1:T(8,128)S(1)} %copy.70), channel_id=1, source_target_pairs={{0,16},{8,24},{16,0},{24,8},{1,17},{9,25},{17,1},{25,9},{2,18},{10... | collective-permute-start | bytes 2193416 | tf_op jit(solution)/shard_map/ppermute | solution.py:23
  90.4 1.5 collective-permute-start
  91.9 15.8 %collective-permute-done.1 = f32[68,21,128]{2,0,1:T(8,128)S(1)} collective-permute-done((f32[68,21,128]{2,0,1:T(8,128)S(1)}, f32[68,21,128]{2,0,1:T(8,128)S(1)}, u32[]{:S(2)}, u32[]{:S(2)}) %collective-permute-start.1) | collective-permute-done | bytes 731168 | tf_op jit(solution)/shard_map/ppermute | solution.py:23
  107.7 1.2 collective-permute-done
  108.9 0.4 copy_add_fusion
  109.4 0.6 collective-permute-start.2
  110.0 1.5 collective-permute-start.3
  111.5 8.0 %collective-permute-done.2 = f32[34,21,128]{2,1,0:T(8,128)S(1)} collective-permute-done((f32[34,21,128]{2,1,0:T(8,128)S(1)}, f32[34,21,128]{2,1,0:T(8,128)S(1)}, u32[]{:S(2)}, u32[]{:S(2)}) %collective-permute-start.2) | collective-permute-done | bytes 365600 | tf_op jit(solution)/shard_map/ppermute | solution.py:23
  119.5 0.3 collective-permute-done.3
  119.8 0.1 select_add_fusion
  119.9 0.1 select_add_fusion.1
  120.0 1.5 collective-permute-start.4
  121.5 1.5 collective-permute-start.5
  123.0 5.9 %collective-permute-done.4 = f32[34,21,128]{2,1,0:T(8,128)S(1)} collective-permute-done((f32[34,21,128]{2,1,0:T(8,128)S(1)}, f32[34,21,128]{2,1,0:T(8,128)S(1)}, u32[]{:S(2)}, u32[]{:S(2)}) %collective-permute-start.4) | collective-permute-done | bytes 365600 | tf_op jit(solution)/shard_map/ppermute | solution.py:23
  128.9 1.4 collective-permute-done.5
  130.3 0.1 maximum_select_fusion.2
  130.4 0.1 maximum_select_fusion.3
  130.5 0.1 copy.73
  130.6 0.1 copy.74
  130.8 0.4 collective-permute-start.7
  131.1 1.5 collective-permute-start.6
  132.6 1.0 copy.84
  133.6 0.1 copy.85
  133.8 11.9 %collective-permute-done.7 = f32[68,21,128]{2,0,1:T(8,128)S(1)} collective-permute-done((f32[68,21,128]{2,0,1:T(8,128)S(1)}, f32[68,21,128]{2,0,1:T(8,128)S(1)}, u32[]{:S(2)}, u32[]{:S(2)}) %collective-permute-start.7) | collective-permute-done | bytes 731168 | tf_op jit(solution)/shard_map/ppermute | solution.py:23
  145.7 0.9 collective-permute-done.6
  146.6 0.0 copy-start.1
  146.6 0.9 copy-done.1
  147.5 0.1 maximum_select_fusion.1
  147.6 0.1 select_n.121
  147.7 2.1 %maximum_select_fusion = f32[2,68,21,128]{3,1,0,2:T(8,128)S(1)} fusion(f32[1,68,21,128]{3,1,0,2:T(8,128)} %bitcast.50, f32[1,68,21,128]{3,1,0,2:T(8,128)} %bitcast.54, pred[]{:T(512)S(6)} %ne.36), kind=kLoop, calls=%fused_computation.7 | loop fusion | flops 1096704 | bytes 2924545 | tf_op jit(solution)/shard_map/jit(_where)/select_n | solution.py:31
  149.9 1.2 select_n.118
  151.1 1.7 %pad_maximum_fusion.1 = f32[256,21,128]{2,0,1:T(8,128)S(1)} fusion(f32[136,21,128]{2,0,1:T(8,128)S(1)} %select_n.121, f32[136,21,128]{2,0,1:T(8,128)} %select_n.118), kind=kLoop, calls=%fused_computation.3 | loop fusion | flops 688128 | bytes 5677056 | tf_op jit(solution)/shard_map/concatenate | solution.py:66
  152.7 0.4 copy.77
  153.2 2.0 %slice_multiply_fusion = f32[64,81,128]{2,0,1:T(8,128)} fusion(f32[64,84,128]{2,0,1:T(8,128)S(1)} %bitcast.44, f32[81,128]{1,0:T(8,128)S(1)} %bitcast.58, f32[64]{0:T(128)S(1)} %slice.97), kind=kLoop, calls=%fused_computation.4 | loop fusion | flops 1990656 | bytes 5350144 | tf_op jit(solution)/shard_map/div | solution.py:19
  (14 shorter events, 0.2 us)
Async XLA Ops:
  7.3 6.5 %copy-start.2 = (s32[24]{0:T(128)S(1)}, s32[24]{0:T(128)}, u32[]{:S(2)}) copy-start(s32[24]{0:T(128)} %param.4) | copy-start | bytes 292
  7.3 6.5 %copy-start = (bf16[64,24,280]{2,1,0:T(8,128)(2,1)S(1)}, bf16[64,24,280]{2,1,0:T(8,128)(2,1)}, u32[]{:S(2)}) copy-start(bf16[64,24,280]{2,1,0:T(8,128)(2,1)} %param.3) | copy-start | bytes 2580484
  7.3 61.1 %all-to-all-start = ((bf16[128,24,280]{2,1,0:T(8,128)(2,1)}), bf16[128,24,280]{2,1,0:T(8,128)(2,1)S(1)}, u32[]{:S(2)}, u32[]{:S(2)}) async-start(bf16[128,24,280]{2,1,0:T(8,128)(2,1)} %copy.62), calls=%async_computation | async-start | bytes 4718592 | tf_op jit(solution)/shard_map/all_to_all | solution.py:97
  88.8 18.9 %collective-permute-start.1 = (f32[68,21,128]{2,0,1:T(8,128)S(1)}, f32[68,21,128]{2,0,1:T(8,128)S(1)}, u32[]{:S(2)}, u32[]{:S(2)}) collective-permute-start(f32[68,21,128]{2,0,1:T(8,128)S(1)} %copy.70), channel_id=1, source_target_pairs={{0,16},{8,24},{16,0},{24,8},{1,17},{9,25},{17,1},{25,9},{2,18},{10... | collective-permute-start | bytes 2193416 | tf_op jit(solution)/shard_map/ppermute | solution.py:23
  90.4 18.5 %collective-permute-start = (f32[68,21,128]{2,0,1:T(8,128)S(1)}, f32[68,21,128]{2,0,1:T(8,128)S(1)}, u32[]{:S(2)}, u32[]{:S(2)}) collective-permute-start(f32[68,21,128]{2,0,1:T(8,128)S(1)} %copy.69), channel_id=1, source_target_pairs={{0,8},{8,0},{16,24},{24,16},{1,9},{9,1},{17,25},{25,17},{2,10},{10... | collective-permute-start | bytes 2193416 | tf_op jit(solution)/shard_map/ppermute | solution.py:23
  109.4 10.0 %collective-permute-start.2 = (f32[34,21,128]{2,1,0:T(8,128)S(1)}, f32[34,21,128]{2,1,0:T(8,128)S(1)}, u32[]{:S(2)}, u32[]{:S(2)}) collective-permute-start(f32[34,21,128]{2,1,0:T(8,128)S(1)} %slice_select_fusion.3), channel_id=1, source_target_pairs={{0,16},{8,24},{16,0},{24,8},{1,17},{9,25},{17,1},{25,9},{2,18},{10... | collective-permute-start | bytes 1096712 | tf_op jit(solution)/shard_map/ppermute | solution.py:23
  110.0 9.8 %collective-permute-start.3 = (f32[34,21,128]{2,1,0:T(8,128)S(1)}, f32[34,21,128]{2,1,0:T(8,128)S(1)}, u32[]{:S(2)}, u32[]{:S(2)}) collective-permute-start(f32[34,21,128]{2,1,0:T(8,128)S(1)} %slice_select_fusion.2), channel_id=1, source_target_pairs={{0,8},{8,0},{16,24},{24,16},{1,9},{9,1},{17,25},{25,17},{2,10},{10... | collective-permute-start | bytes 1096712 | tf_op jit(solution)/shard_map/ppermute | solution.py:23
  120.0 8.9 %collective-permute-start.4 = (f32[34,21,128]{2,1,0:T(8,128)S(1)}, f32[34,21,128]{2,1,0:T(8,128)S(1)}, u32[]{:S(2)}, u32[]{:S(2)}) collective-permute-start(f32[34,21,128]{2,1,0:T(8,128)S(1)} %select_add_fusion.1), channel_id=1, source_target_pairs={{0,16},{8,24},{16,0},{24,8},{1,17},{9,25},{17,1},{25,9},{2,18},{10... | collective-permute-start | bytes 1096712 | tf_op jit(solution)/shard_map/ppermute | solution.py:23
  121.5 8.8 %collective-permute-start.5 = (f32[34,21,128]{2,1,0:T(8,128)S(1)}, f32[34,21,128]{2,1,0:T(8,128)S(1)}, u32[]{:S(2)}, u32[]{:S(2)}) collective-permute-start(f32[34,21,128]{2,1,0:T(8,128)S(1)} %select_add_fusion), channel_id=1, source_target_pairs={{0,8},{8,0},{16,24},{24,16},{1,9},{9,1},{17,25},{25,17},{2,10},{10... | collective-permute-start | bytes 1096712 | tf_op jit(solution)/shard_map/ppermute | solution.py:23
  130.8 14.9 %collective-permute-start.7 = (f32[68,21,128]{2,0,1:T(8,128)S(1)}, f32[68,21,128]{2,0,1:T(8,128)S(1)}, u32[]{:S(2)}, u32[]{:S(2)}) collective-permute-start(f32[68,21,128]{2,0,1:T(8,128)S(1)} %copy.74), channel_id=1, source_target_pairs={{0,16},{8,24},{16,0},{24,8},{1,17},{9,25},{17,1},{25,9},{2,18},{10... | collective-permute-start | bytes 2193416 | tf_op jit(solution)/shard_map/ppermute | solution.py:23
  131.1 15.4 %collective-permute-start.6 = (f32[68,21,128]{2,0,1:T(8,128)S(1)}, f32[68,21,128]{2,0,1:T(8,128)S(1)}, u32[]{:S(2)}, u32[]{:S(2)}) collective-permute-start(f32[68,21,128]{2,0,1:T(8,128)S(1)} %copy.73), channel_id=1, source_target_pairs={{0,8},{8,0},{16,24},{24,16},{1,9},{9,1},{17,25},{25,17},{2,10},{10... | collective-permute-start | bytes 2193416 | tf_op jit(solution)/shard_map/ppermute | solution.py:23
  146.6 0.9 copy-start.1
where the time goes:
time: 156 us; the launch traced here: 155 us
  waiting for transfers between devices  90 us (58%)
  local copies, waits for them, and re-layouts  25.8 us (17%)
  starting transfers between devices  16.4 us (11%)
  matrix products  11.5 us (7%)
  other arithmetic  11.1 us (7%)
    ppermute x8, waiting for transfers between devices, exchange(): return lax.ppermute(value, axis, [(i, i ^ bit) for i in range(size)])  45.5 us
    all_to_all x1, waiting for transfers between devices, body(): lax.all_to_all(outgoing.reshape(slot_count, channels, extent), 'evt', spl...  44.5 us
    conv_general_dilated x1, matrix products, body(): lax.conv_general_dilated(widened, expanded, (fold,), 'VALID', dimension_n...  10.3 us
    ppermute x8, starting transfers between devices, exchange(): return lax.ppermute(value, axis, [(i, i ^ bit) for i in range(size)])  9.99 us
    all_to_all x1, starting transfers between devices, body(): lax.all_to_all(outgoing.reshape(slot_count, channels, extent), 'evt', spl...  6.46 us
    all_to_all x2, local copies, waits for them, and re-layouts, body(): lax.all_to_all(outgoing.reshape(slot_count, channels, extent), 'evt', spl...  5.59 us
    reshape x1, local copies, waits for them, and re-layouts, body(): expanded = jnp.stack(shifted, axis=1).reshape(events * fold, channels, span)  5.22 us
  transfers between devices with their start and end apart: 9, of which 9 were waited for; matrix products, arithmetic and copies ran while one was open for 7% of the time, Pallas kernels for 0%

commit v1 on v0

--- a/solution.py
+++ b/solution.py
@@ -91,11 +91,11 @@
     selection = jnp.dot(slot_hot.T, event_hot, preferred_element_type=jnp.float32).astype(
         jnp.bfloat16
     )
-    outgoing = jnp.dot(
-        selection, traces.reshape(events, channels * extent), preferred_element_type=jnp.float32
+    outgoing = lax.dot_general(
+        selection, traces, (((1,), (0,)), ((), ())), preferred_element_type=jnp.float32
     ).astype(jnp.bfloat16)
     received = lax.all_to_all(
-        outgoing.reshape(slot_count, channels, extent),
+        outgoing,
         "evt",
         split_axis=0,
         concat_axis=0,
@@ -136,7 +136,7 @@
     slot_rows = -(-slot_energy.size // cells)
     energy_rows = -(-events // cells)
     used = events * fold + slot_rows + energy_rows
-    spare = -used % (4 * sta_size)
+    spare = -used % (2 * sta_size)
     flat_slot = jnp.pad(slot_energy.reshape(-1), (0, slot_rows * cells - slot_energy.size))
     flat_event = jnp.pad(event_energy, (0, energy_rows * cells - events))
     packed = jnp.concatenate(

time: 156 us -> 154 us (0.987)
  local copies, waits for them, and re-layouts: 25.8 us -> 23.7 us
    reshape x2 -> x0, local copies, waits for them, and re-layouts: 5.01 us -> none  [the longest x1 2.88 us: body(): outgoing.reshape(slot_count, channels, extent)]
    convert_element_type x0 -> x1, local copies, waits for them, and re-layouts: none -> 2.88 us  [body(): outgoing = lax.dot_general(selection, traces, (((1,), (0,)), ((), ())), p...]
where the time goes in v1:
time: 154 us
  waiting for transfers between devices  89.5 us (58%)
  local copies, waits for them, and re-layouts  23.7 us (15%)
  starting transfers between devices  16.4 us (11%)
  matrix products  12.8 us (8%)
  other arithmetic  11 us (7%)
    ppermute x8, waiting for transfers between devices, exchange(): return lax.ppermute(value, axis, [(i, i ^ bit) for i in range(size)])  45 us
    all_to_all x1, waiting for transfers between devices, body(): lax.all_to_all(outgoing, 'evt', split_axis=0, concat_axis=0, tiled=True)  44.5 us
    conv_general_dilated x1, matrix products, body(): lax.conv_general_dilated(widened, expanded, (fold,), 'VALID', dimension_n...  10.3 us
    ppermute x8, starting transfers between devices, exchange(): return lax.ppermute(value, axis, [(i, i ^ bit) for i in range(size)])  9.98 us
    all_to_all x1, starting transfers between devices, body(): lax.all_to_all(outgoing, 'evt', split_axis=0, concat_axis=0, tiled=True)  6.46 us
    all_to_all x2, local copies, waits for them, and re-layouts, body(): lax.all_to_all(outgoing, 'evt', split_axis=0, concat_axis=0, tiled=True)  5.59 us
    reshape x1, local copies, waits for them, and re-layouts, body(): expanded = jnp.stack(shifted, axis=1).reshape(events * fold, channels, span)  5.22 us
  transfers between devices with their start and end apart: 9, of which 9 were waited for; matrix products, arithmetic and copies ran while one was open for 7% of the time, Pallas kernels for 0%

profile of v1, /device:TPU:0, one launch (start us, length us, event | category | flops | bytes accessed | tf_op | source)
XLA Modules:
  0.0 153.7 jit_solution(11952187554229700999)
XLA Ops:
  0.0 0.8 copy.48
  0.8 0.1 reshape.98
  0.9 0.1 fusion.6
  1.0 0.2 reduce_window_sum.11
  1.2 0.2 select_reduce_fusion
  1.4 2.2 %convolution_convert_fusion = bf16[128,24,280]{0,2,1:T(8,128)(2,1)S(1)} fusion(bf16[64,24,280]{2,1,0:T(8,128)(2,1)} %param.3, s32[128]{0:T(128)S(1)} %get-tuple-element.50, s32[128]{0:T(128)S(1)} %get-tuple-element.51), kind=kOutput, calls=%fused_computation.5 | convolution fusion | flops 113090560 | bytes 2581504 | tf_op jit(solution)/shard_map/dot_general | solution.py:94
  3.6 2.9 %copy.50 = bf16[128,24,280]{2,1,0:T(8,128)(2,1)} copy(bf16[128,24,280]{0,2,1:T(8,128)(2,1)S(1)} %convolution_convert_fusion) | data formatting | bytes 3440640 | tf_op jit(solution)/shard_map/convert_element_type | solution.py:96
  6.5 0.0 copy-start.2
  6.5 0.0 copy-start
  6.5 6.5 %all-to-all-start = ((bf16[128,24,280]{2,1,0:T(8,128)(2,1)}), bf16[128,24,280]{2,1,0:T(8,128)(2,1)S(1)}, u32[]{:S(2)}, u32[]{:S(2)}) async-start(bf16[128,24,280]{2,1,0:T(8,128)(2,1)} %copy.50), calls=%async_computation | async-start | bytes 4718592 | tf_op jit(solution)/shard_map/all_to_all | solution.py:97
  12.9 0.0 copy-done.2
  12.9 0.0 copy-done
  13.0 1.0 multiply_reduce_fusion.1
  13.9 0.9 pad_bitcast_fusion.3
  14.9 0.8 pad_maximum_fusion
  15.7 2.1 %copy.51 = bf16[64,4,24,203]{3,2,1,0:T(8,128)(2,1)} copy(bf16[64,4,24,203]{3,2,0,1:T(8,128)(2,1)S(1)} %pad_maximum_fusion) | data formatting | bytes 4988928 | tf_op jit(solution)/shard_map/stack | solution.py:113
  17.8 5.2 %copy.53 = bf16[256,24,203]{0,1,2:T(8,128)(2,1)} copy(bf16[256,24,203]{2,1,0:T(8,128)(2,1)} %bitcast.44) | data formatting | bytes 4988928 | tf_op jit(solution)/shard_map/reshape | solution.py:113
  23.0 0.1 pad_slice_fusion
  23.1 44.5 %all-to-all-done = bf16[128,24,280]{2,1,0:T(8,128)(2,1)S(1)} async-done(((bf16[128,24,280]{2,1,0:T(8,128)(2,1)}), bf16[128,24,280]{2,1,0:T(8,128)(2,1)S(1)}, u32[]{:S(2)}, u32[]{:S(2)}) %all-to-all-start) | async-done | bytes 1720352 | tf_op jit(solution)/shard_map/all_to_all | solution.py:97
  67.6 2.6 %copy.55 = bf16[128,24,280]{0,2,1:T(8,128)(2,1)} copy(bf16[128,24,280]{2,1,0:T(8,128)(2,1)S(1)} %all-to-all-done) | data formatting | bytes 3440640 | tf_op jit(solution)/shard_map/all_to_all | solution.py:97
  70.2 1.9 %multiply_reduce_fusion = f32[128,280]{0,1:T(8,128)S(1)} fusion(bf16[128,24,280]{0,2,1:T(8,128)(2,1)} %copy.55, f32[24]{0:T(128)S(1)} %get-tuple-element.48), kind=kLoop, calls=%fused_computation | loop fusion | flops 3404800 | bytes 1863776 | tf_op jit(solution)/shard_map/reduce_sum | solution.py:125
  72.2 0.3 convolution_bitcast_fusion
  72.5 3.0 %copy.52 = bf16[128,24,280]{0,1,2:T(8,128)(2,1)} copy(bf16[128,24,280]{2,1,0:T(8,128)(2,1)S(1)} %all-to-all-done) | data formatting | bytes 3440640 | tf_op jit(solution)/shard_map/all_to_all | solution.py:97
  75.5 10.3 %fusion.13 = f32[256,21,128]{2,0,1:T(8,128)S(1)} fusion(bf16[128,24,280]{0,1,2:T(8,128)(2,1)} %copy.52, bf16[256,24,203]{0,1,2:T(8,128)(2,1)} %copy.53), kind=kOutput, calls=%fused_computation.51 | convolution fusion | flops 6700400640 | bytes 6967296 | tf_op jit(solution)/shard_map/conv_general_dilated | solution.py:115
  85.8 1.6 %copy.54 = f32[256,21,128]{2,1,0:T(8,128)S(1)} copy(f32[256,21,128]{2,0,1:T(8,128)S(1)} %fusion.13) | data formatting | bytes 5505024 | tf_op jit(solution)/shard_map/conv_general_dilated | solution.py:115
  87.4 0.3 slice_select_fusion
  87.7 0.1 copy.56
  87.8 0.1 copy.57
  88.0 1.6 %collective-permute-start.1 = (f32[66,21,128]{2,0,1:T(8,128)S(1)}, f32[66,21,128]{2,0,1:T(8,128)S(1)}, u32[]{:S(2)}, u32[]{:S(2)}) collective-permute-start(f32[66,21,128]{2,0,1:T(8,128)S(1)} %copy.57), channel_id=1, source_target_pairs={{0,16},{8,24},{16,0},{24,8},{1,17},{9,25},{17,1},{25,9},{2,18},{10... | collective-permute-start | bytes 2128904 | tf_op jit(solution)/shard_map/ppermute | solution.py:23
  89.6 1.5 collective-permute-start
  91.0 15.8 %collective-permute-done.1 = f32[66,21,128]{2,0,1:T(8,128)S(1)} collective-permute-done((f32[66,21,128]{2,0,1:T(8,128)S(1)}, f32[66,21,128]{2,0,1:T(8,128)S(1)}, u32[]{:S(2)}, u32[]{:S(2)}) %collective-permute-start.1) | collective-permute-done | bytes 709664 | tf_op jit(solution)/shard_map/ppermute | solution.py:23
  106.9 1.2 collective-permute-done
  108.1 0.4 copy_add_fusion
  108.6 0.6 collective-permute-start.2
  109.2 1.5 collective-permute-start.3
  110.7 7.7 %collective-permute-done.2 = f32[33,21,128]{2,1,0:T(8,128)S(1)} collective-permute-done((f32[33,21,128]{2,1,0:T(8,128)S(1)}, f32[33,21,128]{2,1,0:T(8,128)S(1)}, u32[]{:S(2)}, u32[]{:S(2)}) %collective-permute-start.2) | collective-permute-done | bytes 354848 | tf_op jit(solution)/shard_map/ppermute | solution.py:23
  118.4 0.3 collective-permute-done.3
  118.7 0.1 select_add_fusion
  118.8 0.1 select_add_fusion.1
  118.8 1.5 collective-permute-start.4
  120.4 1.5 collective-permute-start.5
  121.8 5.7 %collective-permute-done.4 = f32[33,21,128]{2,1,0:T(8,128)S(1)} collective-permute-done((f32[33,21,128]{2,1,0:T(8,128)S(1)}, f32[33,21,128]{2,1,0:T(8,128)S(1)}, u32[]{:S(2)}, u32[]{:S(2)}) %collective-permute-start.4) | collective-permute-done | bytes 354848 | tf_op jit(solution)/shard_map/ppermute | solution.py:23
  127.5 1.4 collective-permute-done.5
  128.9 0.1 maximum_select_fusion.2
  129.0 0.1 maximum_select_fusion.3
  129.1 0.1 copy.60
  129.2 0.1 copy.61
  129.4 0.4 collective-permute-start.7
  129.8 1.5 collective-permute-start.6
  131.2 1.0 copy.72
  132.2 0.1 copy.73
  132.4 11.9 %collective-permute-done.7 = f32[66,21,128]{2,0,1:T(8,128)S(1)} collective-permute-done((f32[66,21,128]{2,0,1:T(8,128)S(1)}, f32[66,21,128]{2,0,1:T(8,128)S(1)}, u32[]{:S(2)}, u32[]{:S(2)}) %collective-permute-start.7) | collective-permute-done | bytes 709664 | tf_op jit(solution)/shard_map/ppermute | solution.py:23
  144.3 0.9 collective-permute-done.6
  145.2 0.0 copy-start.1
  145.2 0.9 copy-done.1
  146.1 0.1 maximum_select_fusion.1
  146.2 0.1 select_n.121
  146.3 2.1 %maximum_select_fusion = f32[2,66,21,128]{3,1,0,2:T(8,128)S(1)} fusion(f32[1,66,21,128]{3,1,0,2:T(8,128)} %bitcast.51, f32[1,66,21,128]{3,1,0,2:T(8,128)} %bitcast.55, pred[]{:T(512)S(6)} %ne.36), kind=kLoop, calls=%fused_computation.7 | loop fusion | flops 1064448 | bytes 2838529 | tf_op jit(solution)/shard_map/jit(_where)/select_n | solution.py:31
  148.5 1.2 select_n.118
  149.7 1.7 %pad_maximum_fusion.1 = f32[256,21,128]{2,0,1:T(8,128)S(1)} fusion(f32[132,21,128]{2,0,1:T(8,128)S(1)} %select_n.121, f32[132,21,128]{2,0,1:T(8,128)} %select_n.118), kind=kLoop, calls=%fused_computation.2 | loop fusion | flops 688128 | bytes 5591040 | tf_op jit(solution)/shard_map/concatenate | solution.py:66
  151.3 0.4 copy.64
  151.8 2.0 %slice_multiply_fusion = f32[64,81,128]{2,0,1:T(8,128)} fusion(f32[64,84,128]{2,0,1:T(8,128)S(1)} %bitcast.46, f32[81,128]{1,0:T(8,128)S(1)} %bitcast.59, f32[64]{0:T(128)S(1)} %slice.97), kind=kLoop, calls=%fused_computation.3 | loop fusion | flops 1990656 | bytes 5350144 | tf_op jit(solution)/shard_map/div | solution.py:19
  (14 shorter events, 0.2 us)
Async XLA Ops:
  6.5 6.5 %copy-start.2 = (s32[24]{0:T(128)S(1)}, s32[24]{0:T(128)}, u32[]{:S(2)}) copy-start(s32[24]{0:T(128)} %param.4) | copy-start | bytes 292
  6.5 6.5 %copy-start = (bf16[64,24,280]{2,1,0:T(8,128)(2,1)S(1)}, bf16[64,24,280]{2,1,0:T(8,128)(2,1)}, u32[]{:S(2)}) copy-start(bf16[64,24,280]{2,1,0:T(8,128)(2,1)} %param.3) | copy-start | bytes 2580484
  6.5 61.1 %all-to-all-start = ((bf16[128,24,280]{2,1,0:T(8,128)(2,1)}), bf16[128,24,280]{2,1,0:T(8,128)(2,1)S(1)}, u32[]{:S(2)}, u32[]{:S(2)}) async-start(bf16[128,24,280]{2,1,0:T(8,128)(2,1)} %copy.50), calls=%async_computation | async-start | bytes 4718592 | tf_op jit(solution)/shard_map/all_to_all | solution.py:97
  88.0 18.9 %collective-permute-start.1 = (f32[66,21,128]{2,0,1:T(8,128)S(1)}, f32[66,21,128]{2,0,1:T(8,128)S(1)}, u32[]{:S(2)}, u32[]{:S(2)}) collective-permute-start(f32[66,21,128]{2,0,1:T(8,128)S(1)} %copy.57), channel_id=1, source_target_pairs={{0,16},{8,24},{16,0},{24,8},{1,17},{9,25},{17,1},{25,9},{2,18},{10... | collective-permute-start | bytes 2128904 | tf_op jit(solution)/shard_map/ppermute | solution.py:23
  89.6 18.5 %collective-permute-start = (f32[66,21,128]{2,0,1:T(8,128)S(1)}, f32[66,21,128]{2,0,1:T(8,128)S(1)}, u32[]{:S(2)}, u32[]{:S(2)}) collective-permute-start(f32[66,21,128]{2,0,1:T(8,128)S(1)} %copy.56), channel_id=1, source_target_pairs={{0,8},{8,0},{16,24},{24,16},{1,9},{9,1},{17,25},{25,17},{2,10},{10... | collective-permute-start | bytes 2128904 | tf_op jit(solution)/shard_map/ppermute | solution.py:23
  108.6 9.8 %collective-permute-start.2 = (f32[33,21,128]{2,1,0:T(8,128)S(1)}, f32[33,21,128]{2,1,0:T(8,128)S(1)}, u32[]{:S(2)}, u32[]{:S(2)}) collective-permute-start(f32[33,21,128]{2,1,0:T(8,128)S(1)} %slice_select_fusion.3), channel_id=1, source_target_pairs={{0,16},{8,24},{16,0},{24,8},{1,17},{9,25},{17,1},{25,9},{2,18},{10... | collective-permute-start | bytes 1064456 | tf_op jit(solution)/shard_map/ppermute | solution.py:23
  109.2 9.5 %collective-permute-start.3 = (f32[33,21,128]{2,1,0:T(8,128)S(1)}, f32[33,21,128]{2,1,0:T(8,128)S(1)}, u32[]{:S(2)}, u32[]{:S(2)}) collective-permute-start(f32[33,21,128]{2,1,0:T(8,128)S(1)} %slice_select_fusion.2), channel_id=1, source_target_pairs={{0,8},{8,0},{16,24},{24,16},{1,9},{9,1},{17,25},{25,17},{2,10},{10... | collective-permute-start | bytes 1064456 | tf_op jit(solution)/shard_map/ppermute | solution.py:23
  118.8 8.7 %collective-permute-start.4 = (f32[33,21,128]{2,1,0:T(8,128)S(1)}, f32[33,21,128]{2,1,0:T(8,128)S(1)}, u32[]{:S(2)}, u32[]{:S(2)}) collective-permute-start(f32[33,21,128]{2,1,0:T(8,128)S(1)} %select_add_fusion.1), channel_id=1, source_target_pairs={{0,16},{8,24},{16,0},{24,8},{1,17},{9,25},{17,1},{25,9},{2,18},{10... | collective-permute-start | bytes 1064456 | tf_op jit(solution)/shard_map/ppermute | solution.py:23
  120.4 8.6 %collective-permute-start.5 = (f32[33,21,128]{2,1,0:T(8,128)S(1)}, f32[33,21,128]{2,1,0:T(8,128)S(1)}, u32[]{:S(2)}, u32[]{:S(2)}) collective-permute-start(f32[33,21,128]{2,1,0:T(8,128)S(1)} %select_add_fusion), channel_id=1, source_target_pairs={{0,8},{8,0},{16,24},{24,16},{1,9},{9,1},{17,25},{25,17},{2,10},{10... | collective-permute-start | bytes 1064456 | tf_op jit(solution)/shard_map/ppermute | solution.py:23
  129.4 14.9 %collective-permute-start.7 = (f32[66,21,128]{2,0,1:T(8,128)S(1)}, f32[66,21,128]{2,0,1:T(8,128)S(1)}, u32[]{:S(2)}, u32[]{:S(2)}) collective-permute-start(f32[66,21,128]{2,0,1:T(8,128)S(1)} %copy.61), channel_id=1, source_target_pairs={{0,16},{8,24},{16,0},{24,8},{1,17},{9,25},{17,1},{25,9},{2,18},{10... | collective-permute-start | bytes 2128904 | tf_op jit(solution)/shard_map/ppermute | solution.py:23
  129.8 15.4 %collective-permute-start.6 = (f32[66,21,128]{2,0,1:T(8,128)S(1)}, f32[66,21,128]{2,0,1:T(8,128)S(1)}, u32[]{:S(2)}, u32[]{:S(2)}) collective-permute-start(f32[66,21,128]{2,0,1:T(8,128)S(1)} %copy.60), channel_id=1, source_target_pairs={{0,8},{8,0},{16,24},{24,16},{1,9},{9,1},{17,25},{25,17},{2,10},{10... | collective-permute-start | bytes 2128904 | tf_op jit(solution)/shard_map/ppermute | solution.py:23
  145.2 0.9 copy-start.1

commit v2 on v1

--- a/solution.py
+++ b/solution.py
@@ -81,19 +81,11 @@
     before = jnp.cumsum(owner_hot, axis=0) - owner_hot
     ranking = jnp.sum(before * owner_hot, axis=1)
     target = flat * capacity + ranking
-    slot_hot = (target[:, None] == jnp.arange(slot_count, dtype=jnp.int32)[None, :]).astype(
-        jnp.bfloat16
-    )
+    slot_hot = target[:, None] == jnp.arange(slot_count, dtype=jnp.int32)[None, :]
     row_event = jnp.arange(events * partners, dtype=jnp.int32) // partners
-    event_hot = (row_event[:, None] == jnp.arange(events, dtype=jnp.int32)[None, :]).astype(
-        jnp.bfloat16
-    )
-    selection = jnp.dot(slot_hot.T, event_hot, preferred_element_type=jnp.float32).astype(
-        jnp.bfloat16
-    )
-    outgoing = lax.dot_general(
-        selection, traces, (((1,), (0,)), ((), ())), preferred_element_type=jnp.float32
-    ).astype(jnp.bfloat16)
+    filled = jnp.any(slot_hot, axis=0)
+    source = jnp.sum(jnp.where(slot_hot, row_event[:, None], 0), axis=0)
+    outgoing = jnp.take(traces, source, axis=0) * filled.astype(jnp.bfloat16)[:, None, None]
     received = lax.all_to_all(
         outgoing,
         "evt",
@@ -101,6 +93,7 @@
         concat_axis=0,
         tiled=True,
     )
+    received = with_layout_constraint(received, Layout((2, 1, 0)))
     valid = channel_valid.astype(jnp.bfloat16)
     template = traces[:, :, MAXLAG : MAXLAG + WIN] * valid[None, :, None]
     fold = FOLD

time: 154 us -> 152 us (0.987)
  waiting for transfers between devices: 89.5 us -> 94.1 us
  local copies, waits for them, and re-layouts: 23.7 us -> 19.5 us
  matrix products: 12.8 us -> 10 us
  other arithmetic: 11 us -> 12.7 us
    all_to_all x1, waiting for transfers between devices: 44.5 us -> 47.7 us  [body(): lax.all_to_all(outgoing, 'evt', split_axis=0, concat_axis=0, tiled=True)]
    convert_element_type x1 -> x0, local copies, waits for them, and re-layouts: 2.88 us -> none  [body(): outgoing = lax.dot_general(selection, traces, (((1,), (0,)), ((), ())), p...]
    gather x0 -> x1, local copies, waits for them, and re-layouts: none -> 2.38 us  [body(): jnp.take(traces, source, axis=0)]
    dot_general x1 -> x0, matrix products: 2.21 us -> none  [body(): lax.dot_general(selection, traces, (((1,), (0,)), ((), ())), preferred_el...]
    mul x0 -> x1, other arithmetic: none -> 1.86 us  [body(): jnp.take(traces, source, axis=0)]
    all_to_all x2 -> x1, local copies, waits for them, and re-layouts: 5.59 us -> 3.82 us  [body(): lax.all_to_all(outgoing, 'evt', split_axis=0, concat_axis=0, tiled=True)]
    another operation x2, local copies, waits for them, and re-layouts: 2.98 us -> 1.33 us  [body(): expanded = jnp.stack(shifted, axis=1).reshape(events * fold, channels, span)]
  transfers between devices with their start and end apart: 9 -> 9, of which waited for: 9 -> 8; matrix products, arithmetic and copies ran while one was open for 7% -> 6% of each run, Pallas kernels for 0% -> 0%
where the time goes in v2:
time: 152 us
  waiting for transfers between devices  94.1 us (62%)
  local copies, waits for them, and re-layouts  19.5 us (13%)
  starting transfers between devices  15 us (10%)
  other arithmetic  12.7 us (8%)
  matrix products  10 us (7%)
    all_to_all x1, waiting for transfers between devices, body(): lax.all_to_all(outgoing, 'evt', split_axis=0, concat_axis=0, tiled=True)  47.7 us
    ppermute x8, waiting for transfers between devices, exchange(): return lax.ppermute(value, axis, [(i, i ^ bit) for i in range(size)])  46.5 us
    conv_general_dilated x1, matrix products, body(): lax.conv_general_dilated(widened, expanded, (fold,), 'VALID', dimension_n...  9.7 us
    ppermute x8, starting transfers between devices, exchange(): return lax.ppermute(value, axis, [(i, i ^ bit) for i in range(size)])  8.56 us
    all_to_all x1, starting transfers between devices, body(): lax.all_to_all(outgoing, 'evt', split_axis=0, concat_axis=0, tiled=True)  6.45 us
    reshape x1, local copies, waits for them, and re-layouts, body(): expanded = jnp.stack(shifted, axis=1).reshape(events * fold, channels, span)  3.85 us
    all_to_all x1, local copies, waits for them, and re-layouts, body(): lax.all_to_all(outgoing, 'evt', split_axis=0, concat_axis=0, tiled=True)  3.82 us
  transfers between devices with their start and end apart: 9, of which 8 were waited for; matrix products, arithmetic and copies ran while one was open for 6% of the time, Pallas kernels for 0%

profile of v2, /device:TPU:0, one launch (start us, length us, event | category | flops | bytes accessed | tf_op | source)
XLA Modules:
  0.0 151.7 jit_solution(11945736334787008784)
XLA Ops:
  0.0 0.8 copy.57
  0.8 0.1 reshape.119
  0.9 0.1 fusion.5
  1.0 0.2 reduce_window_sum.11
  1.2 0.2 select_reduce_fusion.1
  1.4 0.1 select_reduce_fusion
  1.5 0.1 fusion.4
  1.6 2.4 %gather_fusion = bf16[128,24,280]{2,1,0:T(8,128)(2,1)S(1)} fusion(bf16[64,24,280]{2,1,0:T(8,128)(2,1)} %param.3, s32[1024]{0:T(1024)S(1)} %pad_clamp_fusion), kind=kCustom, calls=%fused_computation | custom fusion | bytes 3441152 | tf_op jit(solution)/shard_map/jit(_take)/gather | solution.py:88
  4.0 1.9 %select_multiply_fusion = bf16[128,24,280]{2,1,0:T(8,128)(2,1)} fusion(bf16[128,24,280]{2,1,0:T(8,128)(2,1)S(1)} %gather_fusion, pred[128]{0:T(512)(128)(4,1)S(1)} %compare_and_fusion, bf16[128]{0:T(256)(128)(2,1)S(1)} %convert_element_type.38), kind=kLoop, calls=%fused_computation.5 | loop fusion | flops 1720320 | bytes 3441024 | tf_op jit(solution)/shard_map/mul | solution.py:88
  5.9 6.5 %all-to-all-start = ((bf16[128,24,280]{2,1,0:T(8,128)(2,1)}), bf16[128,24,280]{2,1,0:T(8,128)(2,1)}, u32[]{:S(2)}, u32[]{:S(2)}) async-start(bf16[128,24,280]{2,1,0:T(8,128)(2,1)} %select_multiply_fusion), calls=%async_computation | async-start | bytes 4718592 | tf_op jit(solution)/shard_map/all_to_all | solution.py:89
  12.3 0.0 copy-done.4
  12.3 0.0 copy-done
  12.4 1.0 multiply_reduce_fusion.1
  13.3 0.9 pad_bitcast_fusion.3
  14.3 0.8 pad_maximum_fusion
  15.1 0.4 copy.59
  15.5 3.8 %copy.60 = bf16[256,24,203]{0,1,2:T(8,128)(2,1)} copy(bf16[256,24,203]{2,1,0:T(8,128)(2,1)S(1)} %bitcast.44) | data formatting | bytes 4988928 | tf_op jit(solution)/shard_map/reshape | solution.py:106
  19.4 0.1 pad_slice_fusion
  19.5 47.7 %all-to-all-done = bf16[128,24,280]{2,1,0:T(8,128)(2,1)} async-done(((bf16[128,24,280]{2,1,0:T(8,128)(2,1)}), bf16[128,24,280]{2,1,0:T(8,128)(2,1)}, u32[]{:S(2)}, u32[]{:S(2)}) %all-to-all-start) | async-done | bytes 1720352 | tf_op jit(solution)/shard_map/all_to_all | solution.py:89
  67.1 3.8 %copy.58 = bf16[128,24,280]{0,1,2:T(8,128)(2,1)S(1)} copy(bf16[128,24,280]{2,1,0:T(8,128)(2,1)} %all-to-all-done) | data formatting | bytes 3440640 | tf_op jit(solution)/shard_map/all_to_all | solution.py:89
  71.0 0.0 copy-start.1
  71.0 1.2 copy-done.1
  72.1 9.7 %fusion.9 = f32[256,21,128]{2,0,1:T(8,128)S(1)} fusion(bf16[128,24,280]{0,1,2:T(8,128)(2,1)S(1)} %copy.58, bf16[256,24,203]{0,1,2:T(8,128)(2,1)} %copy.60), kind=kOutput, calls=%fused_computation.53 | convolution fusion | flops 6700400640 | bytes 6967296 | tf_op jit(solution)/shard_map/conv_general_dilated | solution.py:108
  81.9 0.0 copy-start.2
  81.9 1.6 %copy.61 = f32[256,21,128]{2,1,0:T(8,128)S(1)} copy(f32[256,21,128]{2,0,1:T(8,128)S(1)} %fusion.9) | data formatting | bytes 5505024 | tf_op jit(solution)/shard_map/conv_general_dilated | solution.py:108
  83.5 0.0 copy-done.2
  83.5 1.2 multiply_reduce_fusion
  84.7 0.3 convolution_bitcast_fusion
  85.1 0.2 slice_select_fusion
  85.3 0.1 copy.62
  85.5 1.6 %collective-permute-start = (f32[66,21,128]{2,0,1:T(8,128)S(1)}, f32[66,21,128]{2,0,1:T(8,128)S(1)}, u32[]{:S(2)}, u32[]{:S(2)}) collective-permute-start(f32[66,21,128]{2,0,1:T(8,128)S(1)} %copy.62), channel_id=1, source_target_pairs={{0,8},{8,0},{16,24},{24,16},{1,9},{9,1},{17,25},{25,17},{2,10},{10... | collective-permute-start | bytes 2128904 | tf_op jit(solution)/shard_map/ppermute | solution.py:23
  87.0 0.1 copy.63
  87.2 1.6 %collective-permute-start.1 = (f32[66,21,128]{2,0,1:T(8,128)S(1)}, f32[66,21,128]{2,0,1:T(8,128)S(1)}, u32[]{:S(2)}, u32[]{:S(2)}) collective-permute-start(f32[66,21,128]{2,0,1:T(8,128)S(1)} %copy.63), channel_id=1, source_target_pairs={{0,16},{8,24},{16,0},{24,8},{1,17},{9,25},{17,1},{25,9},{2,18},{10... | collective-permute-start | bytes 2128904 | tf_op jit(solution)/shard_map/ppermute | solution.py:23
  88.7 15.6 %collective-permute-done = f32[66,21,128]{2,0,1:T(8,128)S(1)} collective-permute-done((f32[66,21,128]{2,0,1:T(8,128)S(1)}, f32[66,21,128]{2,0,1:T(8,128)S(1)}, u32[]{:S(2)}, u32[]{:S(2)}) %collective-permute-start) | collective-permute-done | bytes 709664 | tf_op jit(solution)/shard_map/ppermute | solution.py:23
  104.3 1.4 collective-permute-done.1
  105.8 0.7 copy_add_fusion
  106.6 1.6 %collective-permute-start.2 = (f32[33,21,128]{2,1,0:T(8,128)S(1)}, f32[33,21,128]{2,1,0:T(8,128)S(1)}, u32[]{:S(2)}, u32[]{:S(2)}) collective-permute-start(f32[33,21,128]{2,1,0:T(8,128)S(1)} %slice_select_fusion.3), channel_id=1, source_target_pairs={{0,16},{8,24},{16,0},{24,8},{1,17},{9,25},{17,1},{25,9},{2,18},{10... | collective-permute-start | bytes 1064456 | tf_op jit(solution)/shard_map/ppermute | solution.py:23
  108.1 0.5 collective-permute-start.3
  108.7 7.7 %collective-permute-done.2 = f32[33,21,128]{2,1,0:T(8,128)S(1)} collective-permute-done((f32[33,21,128]{2,1,0:T(8,128)S(1)}, f32[33,21,128]{2,1,0:T(8,128)S(1)}, u32[]{:S(2)}, u32[]{:S(2)}) %collective-permute-start.2) | collective-permute-done | bytes 354848 | tf_op jit(solution)/shard_map/ppermute | solution.py:23
  116.3 1.2 collective-permute-done.3
  117.6 0.1 select_add_fusion
  117.7 0.1 select_add_fusion.1
  117.8 0.6 collective-permute-start.4
  118.3 0.5 collective-permute-start.5
  118.9 7.6 %collective-permute-done.4 = f32[33,21,128]{2,1,0:T(8,128)S(1)} collective-permute-done((f32[33,21,128]{2,1,0:T(8,128)S(1)}, f32[33,21,128]{2,1,0:T(8,128)S(1)}, u32[]{:S(2)}, u32[]{:S(2)}) %collective-permute-start.4) | collective-permute-done | bytes 354848 | tf_op jit(solution)/shard_map/ppermute | solution.py:23
  126.4 1.1 collective-permute-done.5
  127.5 0.1 maximum_select_fusion.3
  127.6 0.1 maximum_select_fusion.2
  127.7 0.1 copy.66
  127.8 0.6 collective-permute-start.6
  128.4 0.1 copy.67
  128.6 1.6 %collective-permute-start.7 = (f32[66,21,128]{2,0,1:T(8,128)S(1)}, f32[66,21,128]{2,0,1:T(8,128)S(1)}, u32[]{:S(2)}, u32[]{:S(2)}) collective-permute-start(f32[66,21,128]{2,0,1:T(8,128)S(1)} %copy.67), channel_id=1, source_target_pairs={{0,16},{8,24},{16,0},{24,8},{1,17},{9,25},{17,1},{25,9},{2,18},{10... | collective-permute-start | bytes 2128904 | tf_op jit(solution)/shard_map/ppermute | solution.py:23
  130.1 1.0 copy.76
  131.2 0.1 copy.77
  131.3 11.9 %collective-permute-done.6 = f32[66,21,128]{2,0,1:T(8,128)S(1)} collective-permute-done((f32[66,21,128]{2,0,1:T(8,128)S(1)}, f32[66,21,128]{2,0,1:T(8,128)S(1)}, u32[]{:S(2)}, u32[]{:S(2)}) %collective-permute-start.6) | collective-permute-done | bytes 709664 | tf_op jit(solution)/shard_map/ppermute | solution.py:23
  143.2 0.0 collective-permute-done.7
  143.2 0.9 copy-done.3
  144.1 0.1 maximum_select_fusion.1
  144.2 0.1 select_n.148
  144.4 2.1 %maximum_select_fusion = f32[2,66,21,128]{3,1,0,2:T(8,128)S(1)} fusion(f32[1,66,21,128]{3,1,0,2:T(8,128)} %bitcast.51, f32[1,66,21,128]{3,1,0,2:T(8,128)} %bitcast.55, pred[]{:T(512)S(6)} %ne.38), kind=kLoop, calls=%fused_computation.8 | loop fusion | flops 1064448 | bytes 2838529 | tf_op jit(solution)/shard_map/jit(_where)/select_n | solution.py:31
  146.5 1.2 select_n.145
  147.7 1.7 %pad_maximum_fusion.1 = f32[256,21,128]{2,0,1:T(8,128)S(1)} fusion(f32[132,21,128]{2,0,1:T(8,128)S(1)} %select_n.148, f32[132,21,128]{2,0,1:T(8,128)} %select_n.145), kind=kLoop, calls=%fused_computation.3 | loop fusion | flops 688128 | bytes 5591040 | tf_op jit(solution)/shard_map/concatenate | solution.py:66
  149.3 0.4 copy.70
  149.8 2.0 %slice_multiply_fusion = f32[64,81,128]{2,0,1:T(8,128)} fusion(f32[64,84,128]{2,0,1:T(8,128)S(1)} %bitcast.46, f32[81,128]{1,0:T(8,128)S(1)} %bitcast.59, f32[64]{0:T(128)S(1)} %slice.99), kind=kLoop, calls=%fused_computation.4 | loop fusion | flops 1990656 | bytes 5350144 | tf_op jit(solution)/shard_map/div | solution.py:19
  (21 shorter events, 0.2 us)
Async XLA Ops:
  5.9 6.5 %copy-start.4 = (s32[24]{0:T(128)S(1)}, s32[24]{0:T(128)}, u32[]{:S(2)}) copy-start(s32[24]{0:T(128)} %param.4) | copy-start | bytes 292
  5.9 6.5 %copy-start = (bf16[64,24,280]{2,1,0:T(8,128)(2,1)S(1)}, bf16[64,24,280]{2,1,0:T(8,128)(2,1)}, u32[]{:S(2)}) copy-start(bf16[64,24,280]{2,1,0:T(8,128)(2,1)} %param.3) | copy-start | bytes 2580484
  5.9 61.2 %all-to-all-start = ((bf16[128,24,280]{2,1,0:T(8,128)(2,1)}), bf16[128,24,280]{2,1,0:T(8,128)(2,1)}, u32[]{:S(2)}, u32[]{:S(2)}) async-start(bf16[128,24,280]{2,1,0:T(8,128)(2,1)} %select_multiply_fusion), calls=%async_computation | async-start | bytes 4718592 | tf_op jit(solution)/shard_map/all_to_all | solution.py:89
  71.0 1.2 copy-start.1
  81.9 1.6 %copy-start.2 = (bf16[128,24,280]{0,1,2:T(8,128)(2,1)S(1)}, bf16[128,24,280]{0,1,2:T(8,128)(2,1)}, u32[]{:S(2)}) copy-start(bf16[128,24,280]{0,1,2:T(8,128)(2,1)} %copy-done.1) | copy-start | bytes 5160964
  85.5 18.9 %collective-permute-start = (f32[66,21,128]{2,0,1:T(8,128)S(1)}, f32[66,21,128]{2,0,1:T(8,128)S(1)}, u32[]{:S(2)}, u32[]{:S(2)}) collective-permute-start(f32[66,21,128]{2,0,1:T(8,128)S(1)} %copy.62), channel_id=1, source_target_pairs={{0,8},{8,0},{16,24},{24,16},{1,9},{9,1},{17,25},{25,17},{2,10},{10... | collective-permute-start | bytes 2128904 | tf_op jit(solution)/shard_map/ppermute | solution.py:23
  87.2 18.6 %collective-permute-start.1 = (f32[66,21,128]{2,0,1:T(8,128)S(1)}, f32[66,21,128]{2,0,1:T(8,128)S(1)}, u32[]{:S(2)}, u32[]{:S(2)}) collective-permute-start(f32[66,21,128]{2,0,1:T(8,128)S(1)} %copy.63), channel_id=1, source_target_pairs={{0,16},{8,24},{16,0},{24,8},{1,17},{9,25},{17,1},{25,9},{2,18},{10... | collective-permute-start | bytes 2128904 | tf_op jit(solution)/shard_map/ppermute | solution.py:23
  106.6 9.8 %collective-permute-start.2 = (f32[33,21,128]{2,1,0:T(8,128)S(1)}, f32[33,21,128]{2,1,0:T(8,128)S(1)}, u32[]{:S(2)}, u32[]{:S(2)}) collective-permute-start(f32[33,21,128]{2,1,0:T(8,128)S(1)} %slice_select_fusion.3), channel_id=1, source_target_pairs={{0,16},{8,24},{16,0},{24,8},{1,17},{9,25},{17,1},{25,9},{2,18},{10... | collective-permute-start | bytes 1064456 | tf_op jit(solution)/shard_map/ppermute | solution.py:23
  108.1 9.4 %collective-permute-start.3 = (f32[33,21,128]{2,1,0:T(8,128)S(1)}, f32[33,21,128]{2,1,0:T(8,128)S(1)}, u32[]{:S(2)}, u32[]{:S(2)}) collective-permute-start(f32[33,21,128]{2,1,0:T(8,128)S(1)} %slice_select_fusion.2), channel_id=1, source_target_pairs={{0,8},{8,0},{16,24},{24,16},{1,9},{9,1},{17,25},{25,17},{2,10},{10... | collective-permute-start | bytes 1064456 | tf_op jit(solution)/shard_map/ppermute | solution.py:23
  117.8 8.7 %collective-permute-start.4 = (f32[33,21,128]{2,1,0:T(8,128)S(1)}, f32[33,21,128]{2,1,0:T(8,128)S(1)}, u32[]{:S(2)}, u32[]{:S(2)}) collective-permute-start(f32[33,21,128]{2,1,0:T(8,128)S(1)} %select_add_fusion.1), channel_id=1, source_target_pairs={{0,16},{8,24},{16,0},{24,8},{1,17},{9,25},{17,1},{25,9},{2,18},{10... | collective-permute-start | bytes 1064456 | tf_op jit(solution)/shard_map/ppermute | solution.py:23
  118.3 9.2 %collective-permute-start.5 = (f32[33,21,128]{2,1,0:T(8,128)S(1)}, f32[33,21,128]{2,1,0:T(8,128)S(1)}, u32[]{:S(2)}, u32[]{:S(2)}) collective-permute-start(f32[33,21,128]{2,1,0:T(8,128)S(1)} %select_add_fusion), channel_id=1, source_target_pairs={{0,8},{8,0},{16,24},{24,16},{1,9},{9,1},{17,25},{25,17},{2,10},{10... | collective-permute-start | bytes 1064456 | tf_op jit(solution)/shard_map/ppermute | solution.py:23
  127.8 15.4 %collective-permute-start.6 = (f32[66,21,128]{2,0,1:T(8,128)S(1)}, f32[66,21,128]{2,0,1:T(8,128)S(1)}, u32[]{:S(2)}, u32[]{:S(2)}) collective-permute-start(f32[66,21,128]{2,0,1:T(8,128)S(1)} %copy.66), channel_id=1, source_target_pairs={{0,8},{8,0},{16,24},{24,16},{1,9},{9,1},{17,25},{25,17},{2,10},{10... | collective-permute-start | bytes 2128904 | tf_op jit(solution)/shard_map/ppermute | solution.py:23
  128.6 14.7 %collective-permute-start.7 = (f32[66,21,128]{2,0,1:T(8,128)S(1)}, f32[66,21,128]{2,0,1:T(8,128)S(1)}, u32[]{:S(2)}, u32[]{:S(2)}) collective-permute-start(f32[66,21,128]{2,0,1:T(8,128)S(1)} %copy.67), channel_id=1, source_target_pairs={{0,16},{8,24},{16,0},{24,8},{1,17},{9,25},{17,1},{25,9},{2,18},{10... | collective-permute-start | bytes 2128904 | tf_op jit(solution)/shard_map/ppermute | solution.py:23
  143.2 0.9 copy-start.3

commit v3 on v2

--- a/solution.py
+++ b/solution.py
@@ -113,7 +113,7 @@
         dimension_numbers=("NCH", "OIH", "CHN"),
         preferred_element_type=jnp.float32,
     )
-    lag_scores = with_layout_constraint(lag_scores, Layout((0, 1, 2)))
+    lag_scores = with_layout_constraint(lag_scores, Layout((1, 0, 2)))
     event_energy = jnp.sum(jnp.square(template.astype(jnp.float32)), axis=(1, 2))
     squares_sum = jnp.sum(
         jnp.square(received.astype(jnp.float32)) * channel_valid.astype(jnp.float32)[None, :, None],

time: 152 us -> 146 us (0.961)
  local copies, waits for them, and re-layouts: 19.5 us -> 15 us
  other arithmetic: 12.7 us -> 9.2 us
  waiting for transfers between devices: 94.1 us -> 95.9 us
    unnamed x11 -> x7, local copies, waits for them, and re-layouts: 2.84 us -> 0.78 us
    select_n x4, other arithmetic: 2.37 us -> 0.34 us  [place(): return jnp.where(upper, jnp.stack([other, mine]), jnp.stack([mine, other]))]
    ppermute x8, waiting for transfers between devices: 46.5 us -> 48.3 us  [exchange(): return lax.ppermute(value, axis, [(i, i ^ bit) for i in range(size)])]
    conv_general_dilated x1 -> x0, local copies, waits for them, and re-layouts: 1.62 us -> none  [body(): lax.conv_general_dilated(widened, expanded, (fold,), 'VALID', dimension_n...]
  transfers between devices with their start and end apart: 9 -> 9, of which waited for: 8 -> 8; matrix products, arithmetic and copies ran while one was open for 6% -> 5% of each run, Pallas kernels for 0% -> 0%
where the time goes in v3:
time: 146 us
  waiting for transfers between devices  95.9 us (66%)
  local copies, waits for them, and re-layouts  15 us (10%)
  starting transfers between devices  15 us (10%)
  matrix products  10.3 us (7%)
  other arithmetic  9.2 us (6%)
    ppermute x8, waiting for transfers between devices, exchange(): return lax.ppermute(value, axis, [(i, i ^ bit) for i in range(size)])  48.3 us
    all_to_all x1, waiting for transfers between devices, body(): lax.all_to_all(outgoing, 'evt', split_axis=0, concat_axis=0, tiled=True)  47.6 us
    conv_general_dilated x1, matrix products, body(): lax.conv_general_dilated(widened, expanded, (fold,), 'VALID', dimension_n...  10 us
    ppermute x8, starting transfers between devices, exchange(): return lax.ppermute(value, axis, [(i, i ^ bit) for i in range(size)])  8.59 us
    all_to_all x1, starting transfers between devices, body(): lax.all_to_all(outgoing, 'evt', split_axis=0, concat_axis=0, tiled=True)  6.46 us
    all_to_all x1, local copies, waits for them, and re-layouts, body(): lax.all_to_all(outgoing, 'evt', split_axis=0, concat_axis=0, tiled=True)  4.54 us
    reshape x1, local copies, waits for them, and re-layouts, body(): expanded = jnp.stack(shifted, axis=1).reshape(events * fold, channels, span)  3.85 us
  transfers between devices with their start and end apart: 9, of which 8 were waited for; matrix products, arithmetic and copies ran while one was open for 5% of the time, Pallas kernels for 0%

profile of v3, /device:TPU:0, one launch (start us, length us, event | category | flops | bytes accessed | tf_op | source)
XLA Modules:
  0.0 145.8 jit_solution(4417192897013409291)
XLA Ops:
  0.0 0.8 copy.54
  0.8 0.1 reshape.119
  0.9 0.1 fusion.5
  1.0 0.2 reduce_window_sum.11
  1.2 0.2 select_reduce_fusion.1
  1.4 0.1 select_reduce_fusion
  1.5 0.1 fusion.4
  1.6 2.4 %gather_fusion = bf16[128,24,280]{2,1,0:T(8,128)(2,1)S(1)} fusion(bf16[64,24,280]{2,1,0:T(8,128)(2,1)} %param.3, s32[1024]{0:T(1024)S(1)} %pad_clamp_fusion), kind=kCustom, calls=%fused_computation | custom fusion | bytes 3441152 | tf_op jit(solution)/shard_map/jit(_take)/gather | solution.py:88
  4.0 1.9 %select_multiply_fusion = bf16[128,24,280]{2,1,0:T(8,128)(2,1)} fusion(bf16[128,24,280]{2,1,0:T(8,128)(2,1)S(1)} %gather_fusion, pred[128]{0:T(512)(128)(4,1)S(1)} %compare_and_fusion, bf16[128]{0:T(256)(128)(2,1)S(1)} %convert_element_type.38), kind=kLoop, calls=%fused_computation.5 | loop fusion | flops 1720320 | bytes 3441024 | tf_op jit(solution)/shard_map/mul | solution.py:88
  5.9 0.0 copy-start.2
  5.9 0.0 copy-start
  5.9 6.5 %all-to-all-start = ((bf16[128,24,280]{2,1,0:T(8,128)(2,1)}), bf16[128,24,280]{2,1,0:T(8,128)(2,1)}, u32[]{:S(2)}, u32[]{:S(2)}) async-start(bf16[128,24,280]{2,1,0:T(8,128)(2,1)} %select_multiply_fusion), calls=%async_computation | async-start | bytes 4718592 | tf_op jit(solution)/shard_map/all_to_all | solution.py:89
  12.3 0.0 copy-done.2
  12.3 0.0 copy-done
  12.4 1.0 multiply_reduce_fusion.1
  13.3 0.9 pad_bitcast_fusion.3
  14.3 0.8 pad_maximum_fusion
  15.1 0.4 copy.56
  15.5 3.8 %copy.57 = bf16[256,24,203]{0,1,2:T(8,128)(2,1)} copy(bf16[256,24,203]{2,1,0:T(8,128)(2,1)S(1)} %bitcast.41) | data formatting | bytes 4988928 | tf_op jit(solution)/shard_map/reshape | solution.py:106
  19.4 0.1 pad_slice_fusion
  19.5 47.6 %all-to-all-done = bf16[128,24,280]{2,1,0:T(8,128)(2,1)} async-done(((bf16[128,24,280]{2,1,0:T(8,128)(2,1)}), bf16[128,24,280]{2,1,0:T(8,128)(2,1)}, u32[]{:S(2)}, u32[]{:S(2)}) %all-to-all-start) | async-done | bytes 1720352 | tf_op jit(solution)/shard_map/all_to_all | solution.py:89
  67.1 4.5 %copy.55 = bf16[128,24,280]{0,1,2:T(8,128)(2,1)} copy(bf16[128,24,280]{2,1,0:T(8,128)(2,1)} %all-to-all-done) | data formatting | bytes 3440640 | tf_op jit(solution)/shard_map/all_to_all | solution.py:89
  71.7 0.0 copy-start.1
  71.7 10.0 %fusion.9 = f32[256,21,128]{2,0,1:T(8,128)S(1)} fusion(bf16[128,24,280]{0,1,2:T(8,128)(2,1)} %copy.55, bf16[256,24,203]{0,1,2:T(8,128)(2,1)} %copy.57), kind=kOutput, calls=%fused_computation.54 | convolution fusion | flops 6700400640 | bytes 6967296 | tf_op jit(solution)/shard_map/conv_general_dilated | solution.py:108
  81.7 0.0 copy-done.1
  81.7 1.2 multiply_reduce_fusion
  82.9 0.3 convolution_bitcast_fusion
  83.3 0.4 slice_select_fusion
  83.7 1.6 %collective-permute-start = (f32[66,21,128]{2,0,1:T(8,128)S(1)}, f32[66,21,128]{2,0,1:T(8,128)S(1)}, u32[]{:S(2)}, u32[]{:S(2)}) collective-permute-start(f32[66,21,128]{2,0,1:T(8,128)S(1)} %get-tuple-element.21), channel_id=1, source_target_pairs={{0,8},{8,0},{16,24},{24,16},{1,9},{9,1},{17,25},{25,17},{2,10},{10... | collective-permute-start | bytes 2128904 | tf_op jit(solution)/shard_map/ppermute | solution.py:23
  85.2 1.5 %collective-permute-start.1 = (f32[66,21,128]{2,0,1:T(8,128)S(1)}, f32[66,21,128]{2,0,1:T(8,128)S(1)}, u32[]{:S(2)}, u32[]{:S(2)}) collective-permute-start(f32[66,21,128]{2,0,1:T(8,128)S(1)} %get-tuple-element.22), channel_id=1, source_target_pairs={{0,16},{8,24},{16,0},{24,8},{1,17},{9,25},{17,1},{25,9},{2,18},{10... | collective-permute-start | bytes 2128904 | tf_op jit(solution)/shard_map/ppermute | solution.py:23
  86.8 15.8 %collective-permute-done = f32[66,21,128]{2,0,1:T(8,128)S(1)} collective-permute-done((f32[66,21,128]{2,0,1:T(8,128)S(1)}, f32[66,21,128]{2,0,1:T(8,128)S(1)}, u32[]{:S(2)}, u32[]{:S(2)}) %collective-permute-start) | collective-permute-done | bytes 709664 | tf_op jit(solution)/shard_map/ppermute | solution.py:23
  102.6 1.2 collective-permute-done.1
  103.8 0.4 select_add_fusion
  104.3 1.6 %collective-permute-start.2 = (f32[33,21,128]{2,0,1:T(8,128)S(1)}, f32[33,21,128]{2,0,1:T(8,128)S(1)}, u32[]{:S(2)}, u32[]{:S(2)}) collective-permute-start(f32[33,21,128]{2,0,1:T(8,128)S(1)} %slice_select_fusion.3), channel_id=1, source_target_pairs={{0,16},{8,24},{16,0},{24,8},{1,17},{9,25},{17,1},{25,9},{2,18},{10... | collective-permute-start | bytes 1064456 | tf_op jit(solution)/shard_map/ppermute | solution.py:23
  105.8 0.5 collective-permute-start.3
  106.4 8.2 %collective-permute-done.2 = f32[33,21,128]{2,0,1:T(8,128)S(1)} collective-permute-done((f32[33,21,128]{2,0,1:T(8,128)S(1)}, f32[33,21,128]{2,0,1:T(8,128)S(1)}, u32[]{:S(2)}, u32[]{:S(2)}) %collective-permute-start.2) | collective-permute-done | bytes 354848 | tf_op jit(solution)/shard_map/ppermute | solution.py:23
  114.6 1.2 collective-permute-done.3
  115.8 0.1 select_add_fusion.2
  115.9 0.1 select_add_fusion.3
  116.0 0.6 collective-permute-start.4
  116.6 0.6 collective-permute-start.5
  117.2 8.0 %collective-permute-done.4 = f32[33,21,128]{2,0,1:T(8,128)S(1)} collective-permute-done((f32[33,21,128]{2,0,1:T(8,128)S(1)}, f32[33,21,128]{2,0,1:T(8,128)S(1)}, u32[]{:S(2)}, u32[]{:S(2)}) %collective-permute-start.4) | collective-permute-done | bytes 354848 | tf_op jit(solution)/shard_map/ppermute | solution.py:23
  125.1 0.9 collective-permute-done.5
  126.0 0.1 maximum_select_fusion.3
  126.0 0.2 copy.60
  126.2 0.1 maximum_select_fusion.2
  126.3 0.2 copy.59
  126.4 0.1 copy.61
  126.6 0.7 collective-permute-start.6
  127.2 0.1 copy.62
  127.4 1.6 %collective-permute-start.7 = (f32[66,21,128]{2,0,1:T(8,128)S(1)}, f32[66,21,128]{2,0,1:T(8,128)S(1)}, u32[]{:S(2)}, u32[]{:S(2)}) collective-permute-start(f32[66,21,128]{2,0,1:T(8,128)S(1)} %copy.62), channel_id=1, source_target_pairs={{0,16},{8,24},{16,0},{24,8},{1,17},{9,25},{17,1},{25,9},{2,18},{10... | collective-permute-start | bytes 2128904 | tf_op jit(solution)/shard_map/ppermute | solution.py:23
  129.0 13.0 %collective-permute-done.6 = f32[66,21,128]{2,0,1:T(8,128)S(1)} collective-permute-done((f32[66,21,128]{2,0,1:T(8,128)S(1)}, f32[66,21,128]{2,0,1:T(8,128)S(1)}, u32[]{:S(2)}, u32[]{:S(2)}) %collective-permute-start.6) | collective-permute-done | bytes 709664 | tf_op jit(solution)/shard_map/ppermute | solution.py:23
  142.0 0.0 collective-permute-done.7
  142.0 0.2 copy.70
  142.1 0.1 maximum_select_fusion.1
  142.3 0.3 copy.66
  142.6 0.2 copy.71
  142.7 0.1 maximum_select_fusion
  142.9 0.3 copy.65
  143.1 0.3 pad_maximum_fusion.1
  143.5 0.4 copy.67
  143.9 2.0 %slice_multiply_fusion = f32[64,81,128]{2,0,1:T(8,128)} fusion(f32[64,84,128]{2,0,1:T(8,128)S(1)} %bitcast.43, f32[81,128]{1,0:T(8,128)S(1)} %bitcast.58, f32[64]{0:T(128)S(1)} %slice.99), kind=kLoop, calls=%fused_computation.4 | loop fusion | flops 1990656 | bytes 5350144 | tf_op jit(solution)/shard_map/div | solution.py:19
  (19 shorter events, 0.2 us)
Async XLA Ops:
  5.9 6.5 %copy-start.2 = (s32[24]{0:T(128)S(1)}, s32[24]{0:T(128)}, u32[]{:S(2)}) copy-start(s32[24]{0:T(128)} %param.4) | copy-start | bytes 292
  5.9 6.5 %copy-start = (bf16[64,24,280]{2,1,0:T(8,128)(2,1)S(1)}, bf16[64,24,280]{2,1,0:T(8,128)(2,1)}, u32[]{:S(2)}) copy-start(bf16[64,24,280]{2,1,0:T(8,128)(2,1)} %param.3) | copy-start | bytes 2580484
  5.9 61.2 %all-to-all-start = ((bf16[128,24,280]{2,1,0:T(8,128)(2,1)}), bf16[128,24,280]{2,1,0:T(8,128)(2,1)}, u32[]{:S(2)}, u32[]{:S(2)}) async-start(bf16[128,24,280]{2,1,0:T(8,128)(2,1)} %select_multiply_fusion), calls=%async_computation | async-start | bytes 4718592 | tf_op jit(solution)/shard_map/all_to_all | solution.py:89
  71.7 10.0 %copy-start.1 = (bf16[128,24,280]{0,1,2:T(8,128)(2,1)S(1)}, bf16[128,24,280]{0,1,2:T(8,128)(2,1)}, u32[]{:S(2)}) copy-start(bf16[128,24,280]{0,1,2:T(8,128)(2,1)} %copy.55) | copy-start | bytes 5160964
  83.7 18.9 %collective-permute-start = (f32[66,21,128]{2,0,1:T(8,128)S(1)}, f32[66,21,128]{2,0,1:T(8,128)S(1)}, u32[]{:S(2)}, u32[]{:S(2)}) collective-permute-start(f32[66,21,128]{2,0,1:T(8,128)S(1)} %get-tuple-element.21), channel_id=1, source_target_pairs={{0,8},{8,0},{16,24},{24,16},{1,9},{9,1},{17,25},{25,17},{2,10},{10... | collective-permute-start | bytes 2128904 | tf_op jit(solution)/shard_map/ppermute | solution.py:23
  85.2 18.5 %collective-permute-start.1 = (f32[66,21,128]{2,0,1:T(8,128)S(1)}, f32[66,21,128]{2,0,1:T(8,128)S(1)}, u32[]{:S(2)}, u32[]{:S(2)}) collective-permute-start(f32[66,21,128]{2,0,1:T(8,128)S(1)} %get-tuple-element.22), channel_id=1, source_target_pairs={{0,16},{8,24},{16,0},{24,8},{1,17},{9,25},{17,1},{25,9},{2,18},{10... | collective-permute-start | bytes 2128904 | tf_op jit(solution)/shard_map/ppermute | solution.py:23
  104.3 10.3 %collective-permute-start.2 = (f32[33,21,128]{2,0,1:T(8,128)S(1)}, f32[33,21,128]{2,0,1:T(8,128)S(1)}, u32[]{:S(2)}, u32[]{:S(2)}) collective-permute-start(f32[33,21,128]{2,0,1:T(8,128)S(1)} %slice_select_fusion.3), channel_id=1, source_target_pairs={{0,16},{8,24},{16,0},{24,8},{1,17},{9,25},{17,1},{25,9},{2,18},{10... | collective-permute-start | bytes 1064456 | tf_op jit(solution)/shard_map/ppermute | solution.py:23
  105.8 10.0 %collective-permute-start.3 = (f32[33,21,128]{2,0,1:T(8,128)S(1)}, f32[33,21,128]{2,0,1:T(8,128)S(1)}, u32[]{:S(2)}, u32[]{:S(2)}) collective-permute-start(f32[33,21,128]{2,0,1:T(8,128)S(1)} %slice_select_fusion.2), channel_id=1, source_target_pairs={{0,8},{8,0},{16,24},{24,16},{1,9},{9,1},{17,25},{25,17},{2,10},{10... | collective-permute-start | bytes 1064456 | tf_op jit(solution)/shard_map/ppermute | solution.py:23
  116.0 9.1 %collective-permute-start.4 = (f32[33,21,128]{2,0,1:T(8,128)S(1)}, f32[33,21,128]{2,0,1:T(8,128)S(1)}, u32[]{:S(2)}, u32[]{:S(2)}) collective-permute-start(f32[33,21,128]{2,0,1:T(8,128)S(1)} %select_add_fusion.3), channel_id=1, source_target_pairs={{0,16},{8,24},{16,0},{24,8},{1,17},{9,25},{17,1},{25,9},{2,18},{10... | collective-permute-start | bytes 1064456 | tf_op jit(solution)/shard_map/ppermute | solution.py:23
  116.6 9.4 %collective-permute-start.5 = (f32[33,21,128]{2,0,1:T(8,128)S(1)}, f32[33,21,128]{2,0,1:T(8,128)S(1)}, u32[]{:S(2)}, u32[]{:S(2)}) collective-permute-start(f32[33,21,128]{2,0,1:T(8,128)S(1)} %select_add_fusion.2), channel_id=1, source_target_pairs={{0,8},{8,0},{16,24},{24,16},{1,9},{9,1},{17,25},{25,17},{2,10},{10... | collective-permute-start | bytes 1064456 | tf_op jit(solution)/shard_map/ppermute | solution.py:23
  126.6 15.4 %collective-permute-start.6 = (f32[66,21,128]{2,0,1:T(8,128)S(1)}, f32[66,21,128]{2,0,1:T(8,128)S(1)}, u32[]{:S(2)}, u32[]{:S(2)}) collective-permute-start(f32[66,21,128]{2,0,1:T(8,128)S(1)} %copy.61), channel_id=1, source_target_pairs={{0,8},{8,0},{16,24},{24,16},{1,9},{9,1},{17,25},{25,17},{2,10},{10... | collective-permute-start | bytes 2128904 | tf_op jit(solution)/shard_map/ppermute | solution.py:23
  127.4 14.6 %collective-permute-start.7 = (f32[66,21,128]{2,0,1:T(8,128)S(1)}, f32[66,21,128]{2,0,1:T(8,128)S(1)}, u32[]{:S(2)}, u32[]{:S(2)}) collective-permute-start(f32[66,21,128]{2,0,1:T(8,128)S(1)} %copy.62), channel_id=1, source_target_pairs={{0,16},{8,24},{16,0},{24,8},{1,17},{9,25},{17,1},{25,9},{2,18},{10... | collective-permute-start | bytes 2128904 | tf_op jit(solution)/shard_map/ppermute | solution.py:23

commit v4 on v3

--- a/solution.py
+++ b/solution.py
@@ -85,7 +85,10 @@
     row_event = jnp.arange(events * partners, dtype=jnp.int32) // partners
     filled = jnp.any(slot_hot, axis=0)
     source = jnp.sum(jnp.where(slot_hot, row_event[:, None], 0), axis=0)
-    outgoing = jnp.take(traces, source, axis=0) * filled.astype(jnp.bfloat16)[:, None, None]
+    padded = jnp.pad(traces, ((0, 1), (0, 0), (0, 0)))
+    outgoing = jnp.take(
+        padded, jnp.where(filled, source, events), axis=0, mode="clip"
+    )
     received = lax.all_to_all(
         outgoing,
         "evt",

time: 146 us -> 146 us (level)
  other arithmetic: 9.2 us -> 7.34 us
    mul x1 -> x0, other arithmetic: 1.85 us -> none  [body(): jnp.take(traces, source, axis=0)]
where the time goes in v4:
time: 146 us; the launch traced here: 145 us
  waiting for transfers between devices  95.9 us (66%)
  local copies, waits for them, and re-layouts  16.3 us (11%)
  starting transfers between devices  15 us (10%)
  matrix products  10.3 us (7%)
  other arithmetic  7.34 us (5%)
    ppermute x8, waiting for transfers between devices, exchange(): return lax.ppermute(value, axis, [(i, i ^ bit) for i in range(size)])  48.3 us
    all_to_all x1, waiting for transfers between devices, body(): lax.all_to_all(outgoing, 'evt', split_axis=0, concat_axis=0, tiled=True)  47.6 us
    conv_general_dilated x1, matrix products, body(): lax.conv_general_dilated(widened, expanded, (fold,), 'VALID', dimension_n...  10 us
    ppermute x8, starting transfers between devices, exchange(): return lax.ppermute(value, axis, [(i, i ^ bit) for i in range(size)])  8.59 us
    all_to_all x1, starting transfers between devices, body(): lax.all_to_all(outgoing, 'evt', split_axis=0, concat_axis=0, tiled=True)  6.46 us
    all_to_all x1, local copies, waits for them, and re-layouts, body(): lax.all_to_all(outgoing, 'evt', split_axis=0, concat_axis=0, tiled=True)  4.54 us
    reshape x1, local copies, waits for them, and re-layouts, body(): expanded = jnp.stack(shifted, axis=1).reshape(events * fold, channels, span)  3.85 us
  transfers between devices with their start and end apart: 9, of which 8 were waited for; matrix products, arithmetic and copies ran while one was open for 5% of the time, Pallas kernels for 0%

profile of v4, /device:TPU:0, one launch (start us, length us, event | category | flops | bytes accessed | tf_op | source)
XLA Modules:
  0.0 145.3 jit_solution(5844679897426929527)
XLA Ops:
  0.0 0.8 copy.54
  0.8 0.1 reshape.111
  0.9 0.1 fusion.5
  1.0 0.2 reduce_window_sum.11
  1.2 0.2 select_reduce_fusion.1
  1.4 0.1 fusion.4
  1.5 0.1 select_reduce_fusion
  1.6 1.4 pad.30
  3.0 2.3 %gather_fusion = bf16[128,24,280]{2,1,0:T(8,128)(2,1)} fusion(bf16[65,24,280]{2,1,0:T(8,128)(2,1)S(1)} %pad.30, s32[1024]{0:T(1024)S(1)} %pad_clamp_fusion), kind=kCustom, calls=%fused_computation | custom fusion | bytes 3441152 | tf_op jit(solution)/shard_map/jit(_take)/gather | solution.py:89
  5.3 0.0 copy-start.2
  5.3 0.0 copy-start.1
  5.3 6.5 %all-to-all-start = ((bf16[128,24,280]{2,1,0:T(8,128)(2,1)}), bf16[128,24,280]{2,1,0:T(8,128)(2,1)}, u32[]{:S(2)}, u32[]{:S(2)}) async-start(bf16[128,24,280]{2,1,0:T(8,128)(2,1)} %gather_fusion), calls=%async_computation | async-start | bytes 4718592 | tf_op jit(solution)/shard_map/all_to_all | solution.py:92
  11.8 0.0 copy-done.2
  11.8 0.0 copy-done.1
  11.8 1.0 multiply_reduce_fusion.1
  12.8 0.9 pad_bitcast_fusion.3
  13.7 0.8 pad_maximum_fusion
  14.6 0.4 copy.56
  15.0 3.8 %copy.57 = bf16[256,24,203]{0,1,2:T(8,128)(2,1)} copy(bf16[256,24,203]{2,1,0:T(8,128)(2,1)S(1)} %bitcast.37) | data formatting | bytes 4988928 | tf_op jit(solution)/shard_map/reshape | solution.py:109
  18.9 0.1 pad_slice_fusion
  19.0 47.6 %all-to-all-done = bf16[128,24,280]{2,1,0:T(8,128)(2,1)} async-done(((bf16[128,24,280]{2,1,0:T(8,128)(2,1)}), bf16[128,24,280]{2,1,0:T(8,128)(2,1)}, u32[]{:S(2)}, u32[]{:S(2)}) %all-to-all-start) | async-done | bytes 1720352 | tf_op jit(solution)/shard_map/all_to_all | solution.py:92
  66.6 4.5 %copy.55 = bf16[128,24,280]{0,1,2:T(8,128)(2,1)} copy(bf16[128,24,280]{2,1,0:T(8,128)(2,1)} %all-to-all-done) | data formatting | bytes 3440640 | tf_op jit(solution)/shard_map/all_to_all | solution.py:92
  71.1 0.0 copy-start
  71.1 10.0 %fusion.8 = f32[256,21,128]{2,0,1:T(8,128)S(1)} fusion(bf16[128,24,280]{0,1,2:T(8,128)(2,1)} %copy.55, bf16[256,24,203]{0,1,2:T(8,128)(2,1)} %copy.57), kind=kOutput, calls=%fused_computation.50 | convolution fusion | flops 6700400640 | bytes 6967296 | tf_op jit(solution)/shard_map/conv_general_dilated | solution.py:111
  81.1 0.0 copy-done
  81.2 1.2 multiply_reduce_fusion
  82.3 0.3 convolution_bitcast_fusion
  82.7 0.4 slice_select_fusion
  83.1 1.6 %collective-permute-start = (f32[66,21,128]{2,0,1:T(8,128)S(1)}, f32[66,21,128]{2,0,1:T(8,128)S(1)}, u32[]{:S(2)}, u32[]{:S(2)}) collective-permute-start(f32[66,21,128]{2,0,1:T(8,128)S(1)} %get-tuple-element.21), channel_id=1, source_target_pairs={{0,8},{8,0},{16,24},{24,16},{1,9},{9,1},{17,25},{25,17},{2,10},{10... | collective-permute-start | bytes 2128904 | tf_op jit(solution)/shard_map/ppermute | solution.py:23
  84.7 1.5 %collective-permute-start.1 = (f32[66,21,128]{2,0,1:T(8,128)S(1)}, f32[66,21,128]{2,0,1:T(8,128)S(1)}, u32[]{:S(2)}, u32[]{:S(2)}) collective-permute-start(f32[66,21,128]{2,0,1:T(8,128)S(1)} %get-tuple-element.22), channel_id=1, source_target_pairs={{0,16},{8,24},{16,0},{24,8},{1,17},{9,25},{17,1},{25,9},{2,18},{10... | collective-permute-start | bytes 2128904 | tf_op jit(solution)/shard_map/ppermute | solution.py:23
  86.2 15.8 %collective-permute-done = f32[66,21,128]{2,0,1:T(8,128)S(1)} collective-permute-done((f32[66,21,128]{2,0,1:T(8,128)S(1)}, f32[66,21,128]{2,0,1:T(8,128)S(1)}, u32[]{:S(2)}, u32[]{:S(2)}) %collective-permute-start) | collective-permute-done | bytes 709664 | tf_op jit(solution)/shard_map/ppermute | solution.py:23
  102.0 1.2 collective-permute-done.1
  103.2 0.4 select_add_fusion
  103.7 1.6 %collective-permute-start.2 = (f32[33,21,128]{2,0,1:T(8,128)S(1)}, f32[33,21,128]{2,0,1:T(8,128)S(1)}, u32[]{:S(2)}, u32[]{:S(2)}) collective-permute-start(f32[33,21,128]{2,0,1:T(8,128)S(1)} %slice_select_fusion.3), channel_id=1, source_target_pairs={{0,16},{8,24},{16,0},{24,8},{1,17},{9,25},{17,1},{25,9},{2,18},{10... | collective-permute-start | bytes 1064456 | tf_op jit(solution)/shard_map/ppermute | solution.py:23
  105.3 0.5 collective-permute-start.3
  105.8 8.2 %collective-permute-done.2 = f32[33,21,128]{2,0,1:T(8,128)S(1)} collective-permute-done((f32[33,21,128]{2,0,1:T(8,128)S(1)}, f32[33,21,128]{2,0,1:T(8,128)S(1)}, u32[]{:S(2)}, u32[]{:S(2)}) %collective-permute-start.2) | collective-permute-done | bytes 354848 | tf_op jit(solution)/shard_map/ppermute | solution.py:23
  114.0 1.2 collective-permute-done.3
  115.3 0.1 select_add_fusion.2
  115.4 0.1 select_add_fusion.3
  115.5 0.6 collective-permute-start.4
  116.0 0.6 collective-permute-start.5
  116.6 7.9 %collective-permute-done.4 = f32[33,21,128]{2,0,1:T(8,128)S(1)} collective-permute-done((f32[33,21,128]{2,0,1:T(8,128)S(1)}, f32[33,21,128]{2,0,1:T(8,128)S(1)}, u32[]{:S(2)}, u32[]{:S(2)}) %collective-permute-start.4) | collective-permute-done | bytes 354848 | tf_op jit(solution)/shard_map/ppermute | solution.py:23
  124.6 0.9 collective-permute-done.5
  125.4 0.1 maximum_select_fusion.3
  125.5 0.2 copy.60
  125.6 0.1 maximum_select_fusion.2
  125.7 0.2 copy.59
  125.9 0.1 copy.61
  126.0 0.7 collective-permute-start.6
  126.7 0.1 copy.62
  126.8 1.6 %collective-permute-start.7 = (f32[66,21,128]{2,0,1:T(8,128)S(1)}, f32[66,21,128]{2,0,1:T(8,128)S(1)}, u32[]{:S(2)}, u32[]{:S(2)}) collective-permute-start(f32[66,21,128]{2,0,1:T(8,128)S(1)} %copy.62), channel_id=1, source_target_pairs={{0,16},{8,24},{16,0},{24,8},{1,17},{9,25},{17,1},{25,9},{2,18},{10... | collective-permute-start | bytes 2128904 | tf_op jit(solution)/shard_map/ppermute | solution.py:23
  128.4 13.0 %collective-permute-done.6 = f32[66,21,128]{2,0,1:T(8,128)S(1)} collective-permute-done((f32[66,21,128]{2,0,1:T(8,128)S(1)}, f32[66,21,128]{2,0,1:T(8,128)S(1)}, u32[]{:S(2)}, u32[]{:S(2)}) %collective-permute-start.6) | collective-permute-done | bytes 709664 | tf_op jit(solution)/shard_map/ppermute | solution.py:23
  141.4 0.0 collective-permute-done.7
  141.4 0.2 copy.70
  141.6 0.1 maximum_select_fusion.1
  141.7 0.3 copy.66
  142.0 0.2 copy.71
  142.2 0.1 maximum_select_fusion
  142.3 0.3 copy.65
  142.6 0.3 pad_maximum_fusion.1
  142.9 0.4 copy.67
  143.3 2.0 %slice_multiply_fusion = f32[64,81,128]{2,0,1:T(8,128)} fusion(f32[64,84,128]{2,0,1:T(8,128)S(1)} %bitcast.39, f32[81,128]{1,0:T(8,128)S(1)} %bitcast.54, f32[64]{0:T(128)S(1)} %slice.99), kind=kLoop, calls=%fused_computation.4 | loop fusion | flops 1990656 | bytes 5350144 | tf_op jit(solution)/shard_map/div | solution.py:19
  (17 shorter events, 0.2 us)
Async XLA Ops:
  5.3 6.5 %copy-start.2 = (s32[24]{0:T(128)S(1)}, s32[24]{0:T(128)}, u32[]{:S(2)}) copy-start(s32[24]{0:T(128)} %param.4) | copy-start | bytes 292
  5.3 6.5 %copy-start.1 = (bf16[64,24,280]{2,1,0:T(8,128)(2,1)S(1)}, bf16[64,24,280]{2,1,0:T(8,128)(2,1)}, u32[]{:S(2)}) copy-start(bf16[64,24,280]{2,1,0:T(8,128)(2,1)} %param.3) | copy-start | bytes 2580484
  5.3 61.3 %all-to-all-start = ((bf16[128,24,280]{2,1,0:T(8,128)(2,1)}), bf16[128,24,280]{2,1,0:T(8,128)(2,1)}, u32[]{:S(2)}, u32[]{:S(2)}) async-start(bf16[128,24,280]{2,1,0:T(8,128)(2,1)} %gather_fusion), calls=%async_computation | async-start | bytes 4718592 | tf_op jit(solution)/shard_map/all_to_all | solution.py:92
  71.1 10.0 %copy-start = (bf16[128,24,280]{0,1,2:T(8,128)(2,1)S(1)}, bf16[128,24,280]{0,1,2:T(8,128)(2,1)}, u32[]{:S(2)}) copy-start(bf16[128,24,280]{0,1,2:T(8,128)(2,1)} %copy.55) | copy-start | bytes 5160964
  83.1 18.9 %collective-permute-start = (f32[66,21,128]{2,0,1:T(8,128)S(1)}, f32[66,21,128]{2,0,1:T(8,128)S(1)}, u32[]{:S(2)}, u32[]{:S(2)}) collective-permute-start(f32[66,21,128]{2,0,1:T(8,128)S(1)} %get-tuple-element.21), channel_id=1, source_target_pairs={{0,8},{8,0},{16,24},{24,16},{1,9},{9,1},{17,25},{25,17},{2,10},{10... | collective-permute-start | bytes 2128904 | tf_op jit(solution)/shard_map/ppermute | solution.py:23
  84.7 18.5 %collective-permute-start.1 = (f32[66,21,128]{2,0,1:T(8,128)S(1)}, f32[66,21,128]{2,0,1:T(8,128)S(1)}, u32[]{:S(2)}, u32[]{:S(2)}) collective-permute-start(f32[66,21,128]{2,0,1:T(8,128)S(1)} %get-tuple-element.22), channel_id=1, source_target_pairs={{0,16},{8,24},{16,0},{24,8},{1,17},{9,25},{17,1},{25,9},{2,18},{10... | collective-permute-start | bytes 2128904 | tf_op jit(solution)/shard_map/ppermute | solution.py:23
  103.7 10.3 %collective-permute-start.2 = (f32[33,21,128]{2,0,1:T(8,128)S(1)}, f32[33,21,128]{2,0,1:T(8,128)S(1)}, u32[]{:S(2)}, u32[]{:S(2)}) collective-permute-start(f32[33,21,128]{2,0,1:T(8,128)S(1)} %slice_select_fusion.3), channel_id=1, source_target_pairs={{0,16},{8,24},{16,0},{24,8},{1,17},{9,25},{17,1},{25,9},{2,18},{10... | collective-permute-start | bytes 1064456 | tf_op jit(solution)/shard_map/ppermute | solution.py:23
  105.3 10.0 %collective-permute-start.3 = (f32[33,21,128]{2,0,1:T(8,128)S(1)}, f32[33,21,128]{2,0,1:T(8,128)S(1)}, u32[]{:S(2)}, u32[]{:S(2)}) collective-permute-start(f32[33,21,128]{2,0,1:T(8,128)S(1)} %slice_select_fusion.2), channel_id=1, source_target_pairs={{0,8},{8,0},{16,24},{24,16},{1,9},{9,1},{17,25},{25,17},{2,10},{10... | collective-permute-start | bytes 1064456 | tf_op jit(solution)/shard_map/ppermute | solution.py:23
  115.5 9.1 %collective-permute-start.4 = (f32[33,21,128]{2,0,1:T(8,128)S(1)}, f32[33,21,128]{2,0,1:T(8,128)S(1)}, u32[]{:S(2)}, u32[]{:S(2)}) collective-permute-start(f32[33,21,128]{2,0,1:T(8,128)S(1)} %select_add_fusion.3), channel_id=1, source_target_pairs={{0,16},{8,24},{16,0},{24,8},{1,17},{9,25},{17,1},{25,9},{2,18},{10... | collective-permute-start | bytes 1064456 | tf_op jit(solution)/shard_map/ppermute | solution.py:23
  116.0 9.4 %collective-permute-start.5 = (f32[33,21,128]{2,0,1:T(8,128)S(1)}, f32[33,21,128]{2,0,1:T(8,128)S(1)}, u32[]{:S(2)}, u32[]{:S(2)}) collective-permute-start(f32[33,21,128]{2,0,1:T(8,128)S(1)} %select_add_fusion.2), channel_id=1, source_target_pairs={{0,8},{8,0},{16,24},{24,16},{1,9},{9,1},{17,25},{25,17},{2,10},{10... | collective-permute-start | bytes 1064456 | tf_op jit(solution)/shard_map/ppermute | solution.py:23
  126.0 15.4 %collective-permute-start.6 = (f32[66,21,128]{2,0,1:T(8,128)S(1)}, f32[66,21,128]{2,0,1:T(8,128)S(1)}, u32[]{:S(2)}, u32[]{:S(2)}) collective-permute-start(f32[66,21,128]{2,0,1:T(8,128)S(1)} %copy.61), channel_id=1, source_target_pairs={{0,8},{8,0},{16,24},{24,16},{1,9},{9,1},{17,25},{25,17},{2,10},{10... | collective-permute-start | bytes 2128904 | tf_op jit(solution)/shard_map/ppermute | solution.py:23
  126.8 14.6 %collective-permute-start.7 = (f32[66,21,128]{2,0,1:T(8,128)S(1)}, f32[66,21,128]{2,0,1:T(8,128)S(1)}, u32[]{:S(2)}, u32[]{:S(2)}) collective-permute-start(f32[66,21,128]{2,0,1:T(8,128)S(1)} %copy.62), channel_id=1, source_target_pairs={{0,16},{8,24},{16,0},{24,8},{1,17},{9,25},{17,1},{25,9},{2,18},{10... | collective-permute-start | bytes 2128904 | tf_op jit(solution)/shard_map/ppermute | solution.py:23

commit v5 on v4

--- a/solution.py
+++ b/solution.py
@@ -89,15 +89,8 @@
     outgoing = jnp.take(
         padded, jnp.where(filled, source, events), axis=0, mode="clip"
     )
-    received = lax.all_to_all(
-        outgoing,
-        "evt",
-        split_axis=0,
-        concat_axis=0,
-        tiled=True,
-    )
-    received = with_layout_constraint(received, Layout((2, 1, 0)))
     valid = channel_valid.astype(jnp.bfloat16)
+    valid_wide = channel_valid.astype(jnp.float32)
     template = traces[:, :, MAXLAG : MAXLAG + WIN] * valid[None, :, None]
     fold = FOLD
     positions = -(-lag_count // fold)
@@ -107,21 +100,34 @@
         jnp.pad(template, ((0, 0), (0, 0), (d, fold - 1 - d))) for d in range(fold)
     ]
     expanded = jnp.stack(shifted, axis=1).reshape(events * fold, channels, span)
-    widened = jnp.pad(received, ((0, 0), (0, 0), (0, max(0, reach - extent))))
-    lag_scores = lax.conv_general_dilated(
-        widened,
-        expanded,
-        (fold,),
-        "VALID",
-        dimension_numbers=("NCH", "OIH", "CHN"),
-        preferred_element_type=jnp.float32,
-    )
+    event_energy = jnp.sum(jnp.square(template.astype(jnp.float32)), axis=(1, 2))
+    cut = channels // 2 if channels % 2 == 0 else channels
+    bounds = [(0, cut), (cut, channels)] if cut < channels else [(0, channels)]
+    lag_scores = None
+    squares_sum = None
+    received = None
+    for low, high in bounds:
+        sending = outgoing[:, low:high]
+        if received is not None:
+            received, sending = lax.optimization_barrier((received, sending))
+        received = lax.all_to_all(sending, "evt", split_axis=0, concat_axis=0, tiled=True)
+        received = with_layout_constraint(received, Layout((2, 1, 0)))
+        widened = jnp.pad(received, ((0, 0), (0, 0), (0, max(0, reach - extent))))
+        part = lax.conv_general_dilated(
+            widened,
+            expanded[:, low:high],
+            (fold,),
+            "VALID",
+            dimension_numbers=("NCH", "OIH", "CHN"),
+            preferred_element_type=jnp.float32,
+        )
+        part = with_layout_constraint(part, Layout((1, 0, 2)))
+        squares = jnp.sum(
+            jnp.square(received.astype(jnp.float32)) * valid_wide[None, low:high, None], axis=1
+        )
+        lag_scores = part if lag_scores is None else lag_scores + part
+        squares_sum = squares if squares_sum is None else squares_sum + squares
     lag_scores = with_layout_constraint(lag_scores, Layout((1, 0, 2)))
-    event_energy = jnp.sum(jnp.square(template.astype(jnp.float32)), axis=(1, 2))
-    squares_sum = jnp.sum(
-        jnp.square(received.astype(jnp.float32)) * channel_valid.astype(jnp.float32)[None, :, None],
-        axis=1,
-    )
     slot_energy = lax.dot_general(
         band_table(extent, lag_count),
         squares_sum,

time: 146 us -> 170 us (1.16)
  local copies, waits for them, and re-layouts: 16.3 us -> 26 us
  waiting for transfers between devices: 95.9 us -> 102 us
  matrix products: 10.3 us -> 14.9 us
  starting transfers between devices: 15 us -> 18.6 us
    unnamed x7 -> x9, local copies, waits for them, and re-layouts: 0.78 us -> 8.89 us
    all_to_all x1 -> x2, waiting for transfers between devices: 47.6 us -> 53.4 us  [body(): lax.all_to_all(sending, 'evt', split_axis=0, concat_axis=0, tiled=True)]
    slice x0 -> x3, local copies, waits for them, and re-layouts: none -> 4.75 us  [the longest x1 2.38 us: body(): expanded[:, low:high]]
    conv_general_dilated x1 -> x2, matrix products: 10 us -> 14.5 us  [body(): lax.conv_general_dilated(widened, expanded[:, low:high], (fold,), 'VALID'...]
    reshape x1 -> x0, local copies, waits for them, and re-layouts: 3.85 us -> none  [body(): expanded = jnp.stack(shifted, axis=1).reshape(events * fold, channels, span)]
    all_to_all x1 -> x2, starting transfers between devices: 6.46 us -> 10.1 us  [body(): lax.all_to_all(sending, 'evt', split_axis=0, concat_axis=0, tiled=True)]
    all_to_all x1 -> x2, local copies, waits for them, and re-layouts: 4.54 us -> 4.14 us  [body(): lax.all_to_all(sending, 'evt', split_axis=0, concat_axis=0, tiled=True)]
  transfers between devices with their start and end apart: 9 -> 10, of which waited for: 8 -> 9; matrix products, arithmetic and copies ran while one was open for 5% -> 13% of each run, Pallas kernels for 0% -> 0%
where the time goes in v5:
time: 170 us
  waiting for transfers between devices  102 us (60%)
  local copies, waits for them, and re-layouts  26 us (15%)
  starting transfers between devices  18.6 us (11%)
  matrix products  14.9 us (9%)
  other arithmetic  8.17 us (5%)
    all_to_all x2, waiting for transfers between devices, body(): lax.all_to_all(sending, 'evt', split_axis=0, concat_axis=0, tiled=True)  53.4 us
    ppermute x8, waiting for transfers between devices, exchange(): return lax.ppermute(value, axis, [(i, i ^ bit) for i in range(size)])  48.2 us
    conv_general_dilated x2, matrix products, body(): lax.conv_general_dilated(widened, expanded[:, low:high], (fold,), 'VALID'...  14.5 us
    all_to_all x2, starting transfers between devices, body(): lax.all_to_all(sending, 'evt', split_axis=0, concat_axis=0, tiled=True)  10.1 us
    unnamed x9, local copies, waits for them, and re-layouts  8.89 us
    ppermute x8, starting transfers between devices, exchange(): return lax.ppermute(value, axis, [(i, i ^ bit) for i in range(size)])  8.59 us
    all_to_all x2, local copies, waits for them, and re-layouts, body(): lax.all_to_all(sending, 'evt', split_axis=0, concat_axis=0, tiled=True)  4.14 us
  transfers between devices with their start and end apart: 10, of which 9 were waited for; matrix products, arithmetic and copies ran while one was open for 13% of the time, Pallas kernels for 0%

profile of v5, /device:TPU:0, one launch (start us, length us, event | category | flops | bytes accessed | tf_op | source)
XLA Modules:
  0.0 169.7 jit_solution(4623992334932018012)
XLA Ops:
  0.0 0.8 copy.63
  0.8 0.1 reshape.112
  0.9 0.1 fusion.6
  1.0 0.2 reduce_window_sum.11
  1.2 0.2 select_reduce_fusion.1
  1.4 0.1 fusion.5
  1.5 0.1 select_reduce_fusion
  1.6 2.4 %pad.31 = bf16[65,24,280]{2,1,0:T(8,128)(2,1)} pad(bf16[64,24,280]{2,1,0:T(8,128)(2,1)} %param.3, bf16[]{:T(256)} %constant.36.clone.1), padding=0_1x0_0x0_0 | pad | bytes 1733762 | tf_op jit(solution)/shard_map/jit(_pad)/pad | solution.py:88
  4.0 2.4 %gather_fusion = bf16[128,24,280]{2,1,0:T(8,128)(2,1)S(1)} fusion(bf16[65,24,280]{2,1,0:T(8,128)(2,1)} %pad.31, s32[1024]{0:T(1024)S(1)} %pad_clamp_fusion), kind=kCustom, calls=%fused_computation | custom fusion | bytes 3441152 | tf_op jit(solution)/shard_map/jit(_take)/gather | solution.py:89
  6.4 2.3 %fusion.9 = (bf16[128,12,280]{2,1,0:T(8,128)(2,1)}, bf16[128,12,280]{2,1,0:T(8,128)(2,1)}) fusion(bf16[128,24,280]{2,1,0:T(8,128)(2,1)S(1)} %gather_fusion), kind=kLoop, calls=%fused_computation.53 | loop fusion | bytes 3440640 | tf_op jit(solution)/shard_map/slice | solution.py:110
  8.7 6.5 %all-to-all-start = ((bf16[128,12,280]{2,1,0:T(8,128)(2,1)}), bf16[128,12,280]{2,1,0:T(8,128)(2,1)}, u32[]{:S(2)}, u32[]{:S(2)}) async-start(bf16[128,12,280]{2,1,0:T(8,128)(2,1)} %get-tuple-element.49), calls=%async_computation | async-start | bytes 3145728 | tf_op jit(solution)/shard_map/all_to_all | solution.py:113
  15.2 1.0 multiply_reduce_fusion.2
  16.2 0.9 pad_bitcast_fusion.3
  17.1 0.8 pad_maximum_fusion
  17.9 0.4 copy.65
  18.4 2.4 %fusion.8 = (bf16[256,12,203]{2,1,0:T(8,128)(2,1)S(1)}, bf16[256,12,203]{2,1,0:T(8,128)(2,1)}) fusion(bf16[256,24,203]{2,1,0:T(8,128)(2,1)S(1)} %bitcast.38), kind=kLoop, calls=%fused_computation.52 | loop fusion | bytes 4988928 | tf_op jit(solution)/shard_map/slice | solution.py:118
  20.8 4.8 %copy.79 = bf16[256,12,203]{0,1,2:T(8,128)(2,1)} copy(bf16[256,12,203]{2,1,0:T(8,128)(2,1)} %get-tuple-element.44) | data formatting | bytes 2494464
  25.6 3.2 %copy.80 = bf16[256,12,203]{0,1,2:T(8,128)(2,1)} copy(bf16[256,12,203]{2,1,0:T(8,128)(2,1)S(1)} %get-tuple-element.43) | data formatting | bytes 2494464
  28.8 24.3 %all-to-all-done = bf16[128,12,280]{2,1,0:T(8,128)(2,1)} async-done(((bf16[128,12,280]{2,1,0:T(8,128)(2,1)}), bf16[128,12,280]{2,1,0:T(8,128)(2,1)}, u32[]{:S(2)}, u32[]{:S(2)}) %all-to-all-start) | async-done | bytes 860192 | tf_op jit(solution)/shard_map/all_to_all | solution.py:113
  53.1 2.5 %copy.64 = bf16[128,12,280]{0,1,2:T(8,128)(2,1)S(1)} copy(bf16[128,12,280]{2,1,0:T(8,128)(2,1)} %all-to-all-done) | data formatting | bytes 1720320 | tf_op jit(solution)/shard_map/all_to_all | solution.py:113
  55.6 3.6 %all-to-all-start.1 = ((bf16[128,12,280]{2,1,0:T(8,128)(2,1)}), bf16[128,12,280]{2,1,0:T(8,128)(2,1)S(1)}, u32[]{:S(2)}, u32[]{:S(2)}) async-start(bf16[128,12,280]{2,1,0:T(8,128)(2,1)} %get-tuple-element.22), calls=%async_computation.1 | async-start | bytes 3145728 | tf_op jit(solution)/shard_map/all_to_all | solution.py:113
  59.2 0.1 pad_slice_fusion
  59.3 0.1 fusion.10
  59.4 1.0 multiply_reduce_fusion.1
  60.3 7.6 %fusion.12 = f32[256,21,128]{2,0,1:T(8,128)} fusion(bf16[128,12,280]{0,1,2:T(8,128)(2,1)S(1)} %copy.64, bf16[256,12,203]{0,1,2:T(8,128)(2,1)} %copy.79), kind=kOutput, calls=%fused_computation.56 | convolution fusion | flops 3350200320 | bytes 4859904 | tf_op jit(solution)/shard_map/conv_general_dilated | solution.py:116
  67.9 29.0 %all-to-all-done.1 = bf16[128,12,280]{2,1,0:T(8,128)(2,1)S(1)} async-done(((bf16[128,12,280]{2,1,0:T(8,128)(2,1)}), bf16[128,12,280]{2,1,0:T(8,128)(2,1)S(1)}, u32[]{:S(2)}, u32[]{:S(2)}) %all-to-all-start.1) | async-done | bytes 860192 | tf_op jit(solution)/shard_map/all_to_all | solution.py:113
  97.0 1.6 copy.67
  98.6 0.9 multiply_reduce_fusion
  99.6 0.3 convolution_bitcast_fusion
  99.9 0.1 copy-done.1
  100.0 6.9 %convolution_add_fusion = f32[256,21,128]{2,0,1:T(8,128)S(1)} fusion(f32[256,21,128]{2,0,1:T(8,128)} %fusion.12, bf16[128,12,280]{0,1,2:T(8,128)(2,1)S(1)} %copy.67, bf16[256,12,203]{0,1,2:T(8,128)(2,1)S(1)} %copy-done.1), kind=kOutput, calls=%fused_computation.7 | convolution fusion | flops 3350888448 | bytes 7612416 | tf_op jit(solution)/shard_map/conv_general_dilated | solution.py:116
  107.0 0.4 slice_select_fusion
  107.4 1.6 collective-permute-start
  109.0 1.5 collective-permute-start.1
  110.5 15.8 %collective-permute-done = f32[66,21,128]{2,0,1:T(8,128)S(1)} collective-permute-done((f32[66,21,128]{2,0,1:T(8,128)S(1)}, f32[66,21,128]{2,0,1:T(8,128)S(1)}, u32[]{:S(2)}, u32[]{:S(2)}) %collective-permute-start) | collective-permute-done | bytes 709664 | tf_op jit(solution)/shard_map/ppermute | solution.py:23
  126.3 1.2 collective-permute-done.1
  127.5 0.4 select_add_fusion
  128.1 1.6 collective-permute-start.2
  129.6 0.5 collective-permute-start.3
  130.2 8.2 %collective-permute-done.2 = f32[33,21,128]{2,0,1:T(8,128)S(1)} collective-permute-done((f32[33,21,128]{2,0,1:T(8,128)S(1)}, f32[33,21,128]{2,0,1:T(8,128)S(1)}, u32[]{:S(2)}, u32[]{:S(2)}) %collective-permute-start.2) | collective-permute-done | bytes 354848 | tf_op jit(solution)/shard_map/ppermute | solution.py:23
  138.4 1.2 collective-permute-done.3
  139.6 0.1 select_add_fusion.2
  139.7 0.1 select_add_fusion.3
  139.8 0.6 collective-permute-start.4
  140.4 0.6 collective-permute-start.5
  141.0 7.9 %collective-permute-done.4 = f32[33,21,128]{2,0,1:T(8,128)S(1)} collective-permute-done((f32[33,21,128]{2,0,1:T(8,128)S(1)}, f32[33,21,128]{2,0,1:T(8,128)S(1)}, u32[]{:S(2)}, u32[]{:S(2)}) %collective-permute-start.4) | collective-permute-done | bytes 354848 | tf_op jit(solution)/shard_map/ppermute | solution.py:23
  148.9 0.8 collective-permute-done.5
  149.7 0.1 maximum_select_fusion.3
  149.9 0.2 copy.71
  150.1 0.2 copy.70
  150.2 0.1 copy.72
  150.4 0.7 collective-permute-start.6
  151.1 0.1 copy.73
  151.2 1.6 collective-permute-start.7
  152.8 13.0 %collective-permute-done.6 = f32[66,21,128]{2,0,1:T(8,128)S(1)} collective-permute-done((f32[66,21,128]{2,0,1:T(8,128)S(1)}, f32[66,21,128]{2,0,1:T(8,128)S(1)}, u32[]{:S(2)}, u32[]{:S(2)}) %collective-permute-start.6) | collective-permute-done | bytes 709664 | tf_op jit(solution)/shard_map/ppermute | solution.py:23
  165.8 0.2 copy.83
  166.0 0.1 maximum_select_fusion.1
  166.1 0.3 copy.77
  166.4 0.2 copy.84
  166.6 0.1 maximum_select_fusion
  166.7 0.3 copy.76
  167.0 0.3 pad_maximum_fusion.1
  167.3 0.4 copy.78
  167.7 2.0 %slice_multiply_fusion = f32[64,81,128]{2,0,1:T(8,128)} fusion(f32[64,84,128]{2,0,1:T(8,128)S(1)} %bitcast.40, f32[81,128]{1,0:T(8,128)S(1)} %bitcast.55, f32[64]{0:T(128)S(1)} %slice.127), kind=kLoop, calls=%fused_computation.3 | loop fusion | flops 1990656 | bytes 5350144 | tf_op jit(solution)/shard_map/div | solution.py:19
  (24 shorter events, 0.3 us)
Async XLA Ops:
  8.7 6.5 %copy-start.2 = (s32[24]{0:T(128)S(1)}, s32[24]{0:T(128)}, u32[]{:S(2)}) copy-start(s32[24]{0:T(128)} %param.4) | copy-start | bytes 292
  8.7 6.5 %copy-start = (bf16[64,24,280]{2,1,0:T(8,128)(2,1)S(1)}, bf16[64,24,280]{2,1,0:T(8,128)(2,1)}, u32[]{:S(2)}) copy-start(bf16[64,24,280]{2,1,0:T(8,128)(2,1)} %param.3) | copy-start | bytes 2580484
  8.7 44.4 %all-to-all-start = ((bf16[128,12,280]{2,1,0:T(8,128)(2,1)}), bf16[128,12,280]{2,1,0:T(8,128)(2,1)}, u32[]{:S(2)}, u32[]{:S(2)}) async-start(bf16[128,12,280]{2,1,0:T(8,128)(2,1)} %get-tuple-element.49), calls=%async_computation | async-start | bytes 3145728 | tf_op jit(solution)/shard_map/all_to_all | solution.py:113
  55.6 41.3 %all-to-all-start.1 = ((bf16[128,12,280]{2,1,0:T(8,128)(2,1)}), bf16[128,12,280]{2,1,0:T(8,128)(2,1)S(1)}, u32[]{:S(2)}, u32[]{:S(2)}) async-start(bf16[128,12,280]{2,1,0:T(8,128)(2,1)} %get-tuple-element.22), calls=%async_computation.1 | async-start | bytes 3145728 | tf_op jit(solution)/shard_map/all_to_all | solution.py:113
  98.6 1.4 copy-start.1
  107.4 18.9 %collective-permute-start = (f32[66,21,128]{2,0,1:T(8,128)S(1)}, f32[66,21,128]{2,0,1:T(8,128)S(1)}, u32[]{:S(2)}, u32[]{:S(2)}) collective-permute-start(f32[66,21,128]{2,0,1:T(8,128)S(1)} %get-tuple-element.23), channel_id=1, source_target_pairs={{0,8},{8,0},{16,24},{24,16},{1,9},{9,1},{17,25},{25,17},{2,10},{10... | collective-permute-start | bytes 2128904 | tf_op jit(solution)/shard_map/ppermute | solution.py:23
  109.0 18.5 %collective-permute-start.1 = (f32[66,21,128]{2,0,1:T(8,128)S(1)}, f32[66,21,128]{2,0,1:T(8,128)S(1)}, u32[]{:S(2)}, u32[]{:S(2)}) collective-permute-start(f32[66,21,128]{2,0,1:T(8,128)S(1)} %get-tuple-element.24), channel_id=1, source_target_pairs={{0,16},{8,24},{16,0},{24,8},{1,17},{9,25},{17,1},{25,9},{2,18},{10... | collective-permute-start | bytes 2128904 | tf_op jit(solution)/shard_map/ppermute | solution.py:23
  128.1 10.3 %collective-permute-start.2 = (f32[33,21,128]{2,0,1:T(8,128)S(1)}, f32[33,21,128]{2,0,1:T(8,128)S(1)}, u32[]{:S(2)}, u32[]{:S(2)}) collective-permute-start(f32[33,21,128]{2,0,1:T(8,128)S(1)} %slice_select_fusion.3), channel_id=1, source_target_pairs={{0,16},{8,24},{16,0},{24,8},{1,17},{9,25},{17,1},{25,9},{2,18},{10... | collective-permute-start | bytes 1064456 | tf_op jit(solution)/shard_map/ppermute | solution.py:23
  129.6 10.0 %collective-permute-start.3 = (f32[33,21,128]{2,0,1:T(8,128)S(1)}, f32[33,21,128]{2,0,1:T(8,128)S(1)}, u32[]{:S(2)}, u32[]{:S(2)}) collective-permute-start(f32[33,21,128]{2,0,1:T(8,128)S(1)} %slice_select_fusion.2), channel_id=1, source_target_pairs={{0,8},{8,0},{16,24},{24,16},{1,9},{9,1},{17,25},{25,17},{2,10},{10... | collective-permute-start | bytes 1064456 | tf_op jit(solution)/shard_map/ppermute | solution.py:23
  139.8 9.1 %collective-permute-start.4 = (f32[33,21,128]{2,0,1:T(8,128)S(1)}, f32[33,21,128]{2,0,1:T(8,128)S(1)}, u32[]{:S(2)}, u32[]{:S(2)}) collective-permute-start(f32[33,21,128]{2,0,1:T(8,128)S(1)} %select_add_fusion.3), channel_id=1, source_target_pairs={{0,16},{8,24},{16,0},{24,8},{1,17},{9,25},{17,1},{25,9},{2,18},{10... | collective-permute-start | bytes 1064456 | tf_op jit(solution)/shard_map/ppermute | solution.py:23
  140.4 9.3 %collective-permute-start.5 = (f32[33,21,128]{2,0,1:T(8,128)S(1)}, f32[33,21,128]{2,0,1:T(8,128)S(1)}, u32[]{:S(2)}, u32[]{:S(2)}) collective-permute-start(f32[33,21,128]{2,0,1:T(8,128)S(1)} %select_add_fusion.2), channel_id=1, source_target_pairs={{0,8},{8,0},{16,24},{24,16},{1,9},{9,1},{17,25},{25,17},{2,10},{10... | collective-permute-start | bytes 1064456 | tf_op jit(solution)/shard_map/ppermute | solution.py:23
  150.4 15.4 %collective-permute-start.6 = (f32[66,21,128]{2,0,1:T(8,128)S(1)}, f32[66,21,128]{2,0,1:T(8,128)S(1)}, u32[]{:S(2)}, u32[]{:S(2)}) collective-permute-start(f32[66,21,128]{2,0,1:T(8,128)S(1)} %copy.72), channel_id=1, source_target_pairs={{0,8},{8,0},{16,24},{24,16},{1,9},{9,1},{17,25},{25,17},{2,10},{10... | collective-permute-start | bytes 2128904 | tf_op jit(solution)/shard_map/ppermute | solution.py:23
  151.2 14.6 %collective-permute-start.7 = (f32[66,21,128]{2,0,1:T(8,128)S(1)}, f32[66,21,128]{2,0,1:T(8,128)S(1)}, u32[]{:S(2)}, u32[]{:S(2)}) collective-permute-start(f32[66,21,128]{2,0,1:T(8,128)S(1)} %copy.73), channel_id=1, source_target_pairs={{0,16},{8,24},{16,0},{24,8},{1,17},{9,25},{17,1},{25,9},{2,18},{10... | collective-permute-start | bytes 2128904 | tf_op jit(solution)/shard_map/ppermute | solution.py:23

commit v6 on v4

--- a/solution.py
+++ b/solution.py
@@ -85,16 +85,20 @@
     row_event = jnp.arange(events * partners, dtype=jnp.int32) // partners
     filled = jnp.any(slot_hot, axis=0)
     source = jnp.sum(jnp.where(slot_hot, row_event[:, None], 0), axis=0)
+    evt_index = lax.axis_index("evt")
+    order = jnp.arange(devices_evt, dtype=jnp.int32) ^ evt_index
+    picks = jnp.where(filled, source, events).reshape(devices_evt, capacity)
+    picks = jnp.take(picks, order, axis=0, mode="clip").reshape(-1)
     padded = jnp.pad(traces, ((0, 1), (0, 0), (0, 0)))
-    outgoing = jnp.take(
-        padded, jnp.where(filled, source, events), axis=0, mode="clip"
+    outgoing = jnp.take(padded, picks, axis=0, mode="clip").reshape(
+        devices_evt, capacity, channels, extent
     )
-    received = lax.all_to_all(
-        outgoing,
-        "evt",
-        split_axis=0,
-        concat_axis=0,
-        tiled=True,
+    got = [outgoing[0]] + [
+        lax.ppermute(outgoing[k], "evt", [(i, i ^ k) for i in range(devices_evt)])
+        for k in range(1, devices_evt)
+    ]
+    received = jnp.take(jnp.stack(got), order, axis=0, mode="clip").reshape(
+        slot_count, channels, extent
     )
     received = with_layout_constraint(received, Layout((2, 1, 0)))
     valid = channel_valid.astype(jnp.bfloat16)

time: 146 us -> 150 us (1.027)
  the two profiles are of different devices: /device:TPU:0 before, /device:TPU:16 now
where the time goes in v6:
time: 150 us
  waiting for transfers between devices  83.3 us (56%)
  local copies, waits for them, and re-layouts  32.8 us (22%)
  starting transfers between devices  15.6 us (10%)
  matrix products  10.3 us (7%)
  other arithmetic  7.32 us (5%)
    ppermute x8, waiting for transfers between devices, exchange(): return lax.ppermute(value, axis, [(i, i ^ bit) for i in range(size)])  50.9 us
    ppermute x7, waiting for transfers between devices, body(): lax.ppermute(outgoing[k], 'evt', [(i, i ^ k) for i in range(devices_evt)])  32.4 us
    unnamed x14, local copies, waits for them, and re-layouts  11.8 us
    ppermute x8, starting transfers between devices, exchange(): return lax.ppermute(value, axis, [(i, i ^ bit) for i in range(size)])  10.2 us
    conv_general_dilated x1, matrix products, body(): lax.conv_general_dilated(widened, expanded, (fold,), 'VALID', dimension_n...  10 us
    ppermute x7, starting transfers between devices, body(): lax.ppermute(outgoing[k], 'evt', [(i, i ^ k) for i in range(devices_evt)])  5.42 us
    reshape x1, local copies, waits for them, and re-layouts, body(): expanded = jnp.stack(shifted, axis=1).reshape(events * fold, channels, span)  3.85 us
  transfers between devices with their start and end apart: 15, of which 13 were waited for; matrix products, arithmetic and copies ran while one was open for 12% of the time, Pallas kernels for 0%

profile of v6, /device:TPU:16, one launch (start us, length us, event | category | flops | bytes accessed | tf_op | source)
XLA Modules:
  0.0 149.7 jit_solution(10712846901947730098)
XLA Ops:
  0.0 0.8 copy.40
  1.0 0.2 reduce_window_sum.11
  1.2 0.2 select_reduce_fusion.1
  1.7 0.6 gather_fusion
  2.3 1.4 pad.30
  3.8 2.3 %gather_fusion.1 = bf16[128,24,280]{2,1,0:T(8,128)(2,1)} fusion(bf16[65,24,280]{2,1,0:T(8,128)(2,1)S(1)} %pad.30, s32[1024]{0:T(1024)S(1)} %pad_clamp_fusion), kind=kCustom, calls=%fused_computation.1 | custom fusion | bytes 3441152 | tf_op jit(solution)/shard_map/jit(_take)/gather | solution.py:93
  6.1 2.9 %fusion.8 = (bf16[16,24,280]{2,1,0:T(8,128)(2,1)S(1)}, bf16[16,24,280]{2,1,0:T(8,128)(2,1)}, bf16[16,24,280]{2,1,0:T(8,128)(2,1)}, bf16[16,24,280]{2,1,0:T(8,128...) fusion(bf16[128,24,280]{2,1,0:T(8,128)(2,1)} %gather_fusion.1), kind=kLoop, calls=%fused_computation.62 | loop fusion | bytes 3010560 | tf_op jit(solution)/shard_map/slice | solution.py:97
  8.9 1.6 %collective-permute-start.1 = (bf16[16,24,280]{2,1,0:T(8,128)(2,1)}, bf16[16,24,280]{2,1,0:T(8,128)(2,1)}, u32[]{:S(2)}, u32[]{:S(2)}) collective-permute-start(bf16[16,24,280]{2,1,0:T(8,128)(2,1)} %get-tuple-element.49), channel_id=1, source_target_pairs={{0,2},{1,3},{2,0},{3,1},{4,6},{5,7},{6,4},{7,5},{8,10},{9,11},{10,... | collective-permute-start | bytes 645128 | tf_op jit(solution)/shard_map/ppermute | solution.py:97
  10.5 0.3 collective-permute-start.2
  10.8 0.2 collective-permute-start.3
  11.0 2.3 %collective-permute-start.4 = (bf16[16,24,280]{2,1,0:T(8,128)(2,1)}, bf16[16,24,280]{2,1,0:T(8,128)(2,1)}, u32[]{:S(2)}, u32[]{:S(2)}) collective-permute-start(bf16[16,24,280]{2,1,0:T(8,128)(2,1)} %get-tuple-element.46), channel_id=1, source_target_pairs={{0,5},{1,4},{2,7},{3,6},{4,1},{5,0},{6,3},{7,2},{8,13},{9,12},{10,... | collective-permute-start | bytes 645128 | tf_op jit(solution)/shard_map/ppermute | solution.py:97
  13.4 1.0 multiply_reduce_fusion.1
  14.3 0.9 pad_bitcast_fusion.3
  15.3 0.8 pad_maximum_fusion
  16.1 0.4 copy.42
  16.5 3.8 %copy.43 = bf16[256,24,203]{0,1,2:T(8,128)(2,1)} copy(bf16[256,24,203]{2,1,0:T(8,128)(2,1)S(1)} %bitcast.58) | data formatting | bytes 4988928 | tf_op jit(solution)/shard_map/reshape | solution.py:113
  20.5 1.7 %fusion.1 = bf16[8,16,24,280]{3,2,1,0:T(8,128)(2,1)} fusion(bf16[128,24,280]{2,1,0:T(8,128)(2,1)} %gather_fusion.1), kind=kLoop, calls=%fused_computation.32 | loop fusion | bytes 509952
  22.2 0.5 collective-permute-start.5
  22.7 1.7 %bitcast_dynamic-update-slice_fusion.6 = bf16[8,16,24,280]{3,2,1,0:T(8,128)(2,1)} fusion(bf16[8,16,24,280]{3,2,1,0:T(8,128)(2,1)} %fusion.1, bf16[16,24,280]{2,1,0:T(8,128)(2,1)} %collective-permute-done), kind=kLoop, calls=%fused_computation.39 | loop fusion | bytes 589824
  24.4 3.7 %collective-permute-done.1 = bf16[16,24,280]{2,1,0:T(8,128)(2,1)} collective-permute-done((bf16[16,24,280]{2,1,0:T(8,128)(2,1)}, bf16[16,24,280]{2,1,0:T(8,128)(2,1)}, u32[]{:S(2)}, u32[]{:S(2)}) %collective-permute-start.1) | collective-permute-done | bytes 215072 | tf_op jit(solution)/shard_map/ppermute | solution.py:97
  28.1 0.5 collective-permute-start.6
  28.6 1.7 %bitcast_dynamic-update-slice_fusion.5 = bf16[8,16,24,280]{3,2,1,0:T(8,128)(2,1)} fusion(bf16[8,16,24,280]{3,2,1,0:T(8,128)(2,1)} %bitcast_dynamic-update-slice_fusion.6, bf16[16,24,280]{2,1,0:T(8,128)(2,1)} %collective-permute-done.1), kind=kLoop, calls=%fused_computation.38 | loop fusion | bytes 589824
  30.4 3.7 %collective-permute-done.2 = bf16[16,24,280]{2,1,0:T(8,128)(2,1)} collective-permute-done((bf16[16,24,280]{2,1,0:T(8,128)(2,1)}, bf16[16,24,280]{2,1,0:T(8,128)(2,1)}, u32[]{:S(2)}, u32[]{:S(2)}) %collective-permute-start.2) | collective-permute-done | bytes 215072 | tf_op jit(solution)/shard_map/ppermute | solution.py:97
  34.0 1.7 %bitcast_dynamic-update-slice_fusion.4 = bf16[8,16,24,280]{3,2,1,0:T(8,128)(2,1)} fusion(bf16[8,16,24,280]{3,2,1,0:T(8,128)(2,1)} %bitcast_dynamic-update-slice_fusion.5, bf16[16,24,280]{2,1,0:T(8,128)(2,1)} %collective-permute-done.2), kind=kLoop, calls=%fused_computation.37 | loop fusion | bytes 589824
  35.8 1.7 %bitcast_dynamic-update-slice_fusion.3 = bf16[8,16,24,280]{3,2,1,0:T(8,128)(2,1)} fusion(bf16[8,16,24,280]{3,2,1,0:T(8,128)(2,1)} %bitcast_dynamic-update-slice_fusion.4, bf16[16,24,280]{2,1,0:T(8,128)(2,1)} %collective-permute-done.3), kind=kLoop, calls=%fused_computation.36 | loop fusion | bytes 589824
  37.4 12.8 %collective-permute-done.4 = bf16[16,24,280]{2,1,0:T(8,128)(2,1)} collective-permute-done((bf16[16,24,280]{2,1,0:T(8,128)(2,1)}, bf16[16,24,280]{2,1,0:T(8,128)(2,1)}, u32[]{:S(2)}, u32[]{:S(2)}) %collective-permute-start.4) | collective-permute-done | bytes 215072 | tf_op jit(solution)/shard_map/ppermute | solution.py:97
  50.3 1.7 %bitcast_dynamic-update-slice_fusion.2 = bf16[8,16,24,280]{3,2,1,0:T(8,128)(2,1)} fusion(bf16[8,16,24,280]{3,2,1,0:T(8,128)(2,1)} %bitcast_dynamic-update-slice_fusion.3, bf16[16,24,280]{2,1,0:T(8,128)(2,1)} %collective-permute-done.4), kind=kLoop, calls=%fused_computation.35 | loop fusion | bytes 589824
  52.0 7.8 %collective-permute-done.5 = bf16[16,24,280]{2,1,0:T(8,128)(2,1)S(1)} collective-permute-done((bf16[16,24,280]{2,1,0:T(8,128)(2,1)}, bf16[16,24,280]{2,1,0:T(8,128)(2,1)S(1)}, u32[]{:S(2)}, u32[]{:S(2)}) %collective-permute-start.5) | collective-permute-done | bytes 215072 | tf_op jit(solution)/shard_map/ppermute | solution.py:97
  59.8 0.7 bitcast_dynamic-update-slice_fusion.1
  60.5 4.3 %collective-permute-done.6 = bf16[16,24,280]{2,1,0:T(8,128)(2,1)S(1)} collective-permute-done((bf16[16,24,280]{2,1,0:T(8,128)(2,1)S(1)}, bf16[16,24,280]{2,1,0:T(8,128)(2,1)S(1)}, u32[]{:S(2)}, u32[]{:S(2)}) %collective-permute-start.6) | collective-permute-done | bytes 215072 | tf_op jit(solution)/shard_map/ppermute | solution.py:97
  64.9 0.8 bitcast_dynamic-update-slice_fusion
  65.6 2.7 %gather_fusion.2 = bf16[8,16,24,280]{3,2,1,0:T(8,128)(2,1)S(1)} fusion(bf16[8,16,24,280]{3,2,1,0:T(8,128)(2,1)} %bitcast_dynamic-update-slice_fusion, s32[1024]{0:T(1024)S(1)} %pad_clamp_fusion.1), kind=kCustom, calls=%fused_computation.2 | custom fusion | bytes 3440672 | tf_op jit(solution)/shard_map/jit(_take)/gather | solution.py:100
  68.4 3.0 %copy.41 = bf16[128,24,280]{0,1,2:T(8,128)(2,1)} copy(bf16[128,24,280]{2,1,0:T(8,128)(2,1)S(1)} %bitcast.61) | data formatting | bytes 3440640 | tf_op jit(solution)/shard_map/reshape | solution.py:100
  71.3 10.0 %fusion.10 = f32[256,21,128]{2,0,1:T(8,128)S(1)} fusion(bf16[128,24,280]{0,1,2:T(8,128)(2,1)} %copy.41, bf16[256,24,203]{0,1,2:T(8,128)(2,1)} %copy.43), kind=kOutput, calls=%fused_computation.64 | convolution fusion | flops 6700400640 | bytes 6967296 | tf_op jit(solution)/shard_map/conv_general_dilated | solution.py:115
  81.3 1.2 multiply_reduce_fusion
  82.5 0.3 convolution_bitcast_fusion
  82.9 0.4 slice_select_fusion
  83.3 1.6 %collective-permute-start.7 = (f32[66,21,128]{2,0,1:T(8,128)S(1)}, f32[66,21,128]{2,0,1:T(8,128)S(1)}, u32[]{:S(2)}, u32[]{:S(2)}) collective-permute-start(f32[66,21,128]{2,0,1:T(8,128)S(1)} %get-tuple-element.21), channel_id=1, source_target_pairs={{0,8},{8,0},{16,24},{24,16},{1,9},{9,1},{17,25},{25,17},{2,10},{10... | collective-permute-start | bytes 2128904 | tf_op jit(solution)/shard_map/ppermute | solution.py:23
  84.9 1.5 %collective-permute-start.8 = (f32[66,21,128]{2,0,1:T(8,128)S(1)}, f32[66,21,128]{2,0,1:T(8,128)S(1)}, u32[]{:S(2)}, u32[]{:S(2)}) collective-permute-start(f32[66,21,128]{2,0,1:T(8,128)S(1)} %get-tuple-element.22), channel_id=1, source_target_pairs={{0,16},{8,24},{16,0},{24,8},{1,17},{9,25},{17,1},{25,9},{2,18},{10... | collective-permute-start | bytes 2128904 | tf_op jit(solution)/shard_map/ppermute | solution.py:23
  86.4 16.6 %collective-permute-done.7 = f32[66,21,128]{2,0,1:T(8,128)S(1)} collective-permute-done((f32[66,21,128]{2,0,1:T(8,128)S(1)}, f32[66,21,128]{2,0,1:T(8,128)S(1)}, u32[]{:S(2)}, u32[]{:S(2)}) %collective-permute-start.7) | collective-permute-done | bytes 709664 | tf_op jit(solution)/shard_map/ppermute | solution.py:23
  103.0 1.2 collective-permute-done.8
  104.3 0.4 select_add_fusion
  104.7 0.6 collective-permute-start.10
  105.3 1.5 %collective-permute-start.9 = (f32[33,21,128]{2,0,1:T(8,128)S(1)}, f32[33,21,128]{2,0,1:T(8,128)S(1)}, u32[]{:S(2)}, u32[]{:S(2)}) collective-permute-start(f32[33,21,128]{2,0,1:T(8,128)S(1)} %slice_select_fusion.3), channel_id=1, source_target_pairs={{0,16},{8,24},{16,0},{24,8},{1,17},{9,25},{17,1},{25,9},{2,18},{10... | collective-permute-start | bytes 1064456 | tf_op jit(solution)/shard_map/ppermute | solution.py:23
  106.9 9.1 %collective-permute-done.10 = f32[33,21,128]{2,0,1:T(8,128)S(1)} collective-permute-done((f32[33,21,128]{2,0,1:T(8,128)S(1)}, f32[33,21,128]{2,0,1:T(8,128)S(1)}, u32[]{:S(2)}, u32[]{:S(2)}) %collective-permute-start.10) | collective-permute-done | bytes 354848 | tf_op jit(solution)/shard_map/ppermute | solution.py:23
  116.0 0.3 collective-permute-done.9
  116.4 1.6 %collective-permute-start.11 = (f32[33,21,128]{2,0,1:T(8,128)S(1)}, f32[33,21,128]{2,0,1:T(8,128)S(1)}, u32[]{:S(2)}, u32[]{:S(2)}) collective-permute-start(f32[33,21,128]{2,0,1:T(8,128)S(1)} %select_add_fusion.3), channel_id=1, source_target_pairs={{0,16},{8,24},{16,0},{24,8},{1,17},{9,25},{17,1},{25,9},{2,18},{10... | collective-permute-start | bytes 1064456 | tf_op jit(solution)/shard_map/ppermute | solution.py:23
  118.0 1.4 collective-permute-start.12
  119.5 7.1 %collective-permute-done.11 = f32[33,21,128]{2,0,1:T(8,128)S(1)} collective-permute-done((f32[33,21,128]{2,0,1:T(8,128)S(1)}, f32[33,21,128]{2,0,1:T(8,128)S(1)}, u32[]{:S(2)}, u32[]{:S(2)}) %collective-permute-start.11) | collective-permute-done | bytes 354848 | tf_op jit(solution)/shard_map/ppermute | solution.py:23
  126.5 1.2 collective-permute-done.12
  127.8 0.2 copy.46
  128.1 0.2 copy.45
  128.2 0.1 copy.47
  128.4 1.4 collective-permute-start.13
  130.0 0.6 collective-permute-start.14
  130.5 14.1 %collective-permute-done.13 = f32[66,21,128]{2,0,1:T(8,128)S(1)} collective-permute-done((f32[66,21,128]{2,0,1:T(8,128)S(1)}, f32[66,21,128]{2,0,1:T(8,128)S(1)}, u32[]{:S(2)}, u32[]{:S(2)}) %collective-permute-start.13) | collective-permute-done | bytes 709664 | tf_op jit(solution)/shard_map/ppermute | solution.py:23
  144.7 1.2 collective-permute-done.14
  145.9 0.2 copy.56
  146.2 0.3 copy.52
  146.5 0.2 copy.57
  146.7 0.3 copy.51
  147.0 0.3 pad_maximum_fusion.1
  147.3 0.4 copy.53
  147.8 2.0 %slice_multiply_fusion = f32[64,81,128]{2,0,1:T(8,128)} fusion(f32[64,84,128]{2,0,1:T(8,128)S(1)} %bitcast.60, f32[81,128]{1,0:T(8,128)S(1)} %bitcast.76, f32[64]{0:T(128)S(1)} %slice.154), kind=kLoop, calls=%fused_computation.6 | loop fusion | flops 1990656 | bytes 5350144 | tf_op jit(solution)/shard_map/div | solution.py:19
  (42 shorter events, 1.5 us)
Async XLA Ops:
  6.1 7.3 %copy-start.2 = (s32[24]{0:T(128)S(1)}, s32[24]{0:T(128)}, u32[]{:S(2)}) copy-start(s32[24]{0:T(128)} %param.4) | copy-start | bytes 292
  6.1 7.3 %copy-start.1 = (bf16[64,24,280]{2,1,0:T(8,128)(2,1)S(1)}, bf16[64,24,280]{2,1,0:T(8,128)(2,1)}, u32[]{:S(2)}) copy-start(bf16[64,24,280]{2,1,0:T(8,128)(2,1)} %param.3) | copy-start | bytes 2580484
  8.9 13.3 %collective-permute-start = (bf16[16,24,280]{2,1,0:T(8,128)(2,1)}, bf16[16,24,280]{2,1,0:T(8,128)(2,1)}, u32[]{:S(2)}, u32[]{:S(2)}) collective-permute-start(bf16[16,24,280]{2,1,0:T(8,128)(2,1)} %get-tuple-element.50), channel_id=1, source_target_pairs={{0,1},{1,0},{2,3},{3,2},{4,5},{5,4},{6,7},{7,6},{8,9},{9,8},{10,11... | collective-permute-start | bytes 645128 | tf_op jit(solution)/shard_map/ppermute | solution.py:97
  8.9 19.2 %collective-permute-start.1 = (bf16[16,24,280]{2,1,0:T(8,128)(2,1)}, bf16[16,24,280]{2,1,0:T(8,128)(2,1)}, u32[]{:S(2)}, u32[]{:S(2)}) collective-permute-start(bf16[16,24,280]{2,1,0:T(8,128)(2,1)} %get-tuple-element.49), channel_id=1, source_target_pairs={{0,2},{1,3},{2,0},{3,1},{4,6},{5,7},{6,4},{7,5},{8,10},{9,11},{10,... | collective-permute-start | bytes 645128 | tf_op jit(solution)/shard_map/ppermute | solution.py:97
  10.5 23.5 %collective-permute-start.2 = (bf16[16,24,280]{2,1,0:T(8,128)(2,1)}, bf16[16,24,280]{2,1,0:T(8,128)(2,1)}, u32[]{:S(2)}, u32[]{:S(2)}) collective-permute-start(bf16[16,24,280]{2,1,0:T(8,128)(2,1)} %get-tuple-element.48), channel_id=1, source_target_pairs={{0,3},{1,2},{2,1},{3,0},{4,7},{5,6},{6,5},{7,4},{8,11},{9,10},{10,... | collective-permute-start | bytes 645128 | tf_op jit(solution)/shard_map/ppermute | solution.py:97
  10.8 25.0 %collective-permute-start.3 = (bf16[16,24,280]{2,1,0:T(8,128)(2,1)}, bf16[16,24,280]{2,1,0:T(8,128)(2,1)}, u32[]{:S(2)}, u32[]{:S(2)}) collective-permute-start(bf16[16,24,280]{2,1,0:T(8,128)(2,1)} %get-tuple-element.47), channel_id=1, source_target_pairs={{0,4},{1,5},{2,6},{3,7},{4,0},{5,1},{6,2},{7,3},{8,12},{9,13},{10,... | collective-permute-start | bytes 645128 | tf_op jit(solution)/shard_map/ppermute | solution.py:97
  11.0 39.3 %collective-permute-start.4 = (bf16[16,24,280]{2,1,0:T(8,128)(2,1)}, bf16[16,24,280]{2,1,0:T(8,128)(2,1)}, u32[]{:S(2)}, u32[]{:S(2)}) collective-permute-start(bf16[16,24,280]{2,1,0:T(8,128)(2,1)} %get-tuple-element.46), channel_id=1, source_target_pairs={{0,5},{1,4},{2,7},{3,6},{4,1},{5,0},{6,3},{7,2},{8,13},{9,12},{10,... | collective-permute-start | bytes 645128 | tf_op jit(solution)/shard_map/ppermute | solution.py:97
  22.2 37.6 %collective-permute-start.5 = (bf16[16,24,280]{2,1,0:T(8,128)(2,1)}, bf16[16,24,280]{2,1,0:T(8,128)(2,1)S(1)}, u32[]{:S(2)}, u32[]{:S(2)}) collective-permute-start(bf16[16,24,280]{2,1,0:T(8,128)(2,1)} %get-tuple-element.45), channel_id=1, source_target_pairs={{0,6},{1,7},{2,4},{3,5},{4,2},{5,3},{6,0},{7,1},{8,14},{9,15},{10,... | collective-permute-start | bytes 645128 | tf_op jit(solution)/shard_map/ppermute | solution.py:97
  28.1 36.8 %collective-permute-start.6 = (bf16[16,24,280]{2,1,0:T(8,128)(2,1)S(1)}, bf16[16,24,280]{2,1,0:T(8,128)(2,1)S(1)}, u32[]{:S(2)}, u32[]{:S(2)}) collective-permute-start(bf16[16,24,280]{2,1,0:T(8,128)(2,1)S(1)} %get-tuple-element.44), channel_id=1, source_target_pairs={{0,7},{1,6},{2,5},{3,4},{4,3},{5,2},{6,1},{7,0},{8,15},{9,14},{10,... | collective-permute-start | bytes 645128 | tf_op jit(solution)/shard_map/ppermute | solution.py:97
  71.3 10.0 %copy-start = (bf16[128,24,280]{0,1,2:T(8,128)(2,1)S(1)}, bf16[128,24,280]{0,1,2:T(8,128)(2,1)}, u32[]{:S(2)}) copy-start(bf16[128,24,280]{0,1,2:T(8,128)(2,1)} %copy.41) | copy-start | bytes 5160964
  83.3 19.7 %collective-permute-start.7 = (f32[66,21,128]{2,0,1:T(8,128)S(1)}, f32[66,21,128]{2,0,1:T(8,128)S(1)}, u32[]{:S(2)}, u32[]{:S(2)}) collective-permute-start(f32[66,21,128]{2,0,1:T(8,128)S(1)} %get-tuple-element.21), channel_id=1, source_target_pairs={{0,8},{8,0},{16,24},{24,16},{1,9},{9,1},{17,25},{25,17},{2,10},{10... | collective-permute-start | bytes 2128904 | tf_op jit(solution)/shard_map/ppermute | solution.py:23
  84.9 19.4 %collective-permute-start.8 = (f32[66,21,128]{2,0,1:T(8,128)S(1)}, f32[66,21,128]{2,0,1:T(8,128)S(1)}, u32[]{:S(2)}, u32[]{:S(2)}) collective-permute-start(f32[66,21,128]{2,0,1:T(8,128)S(1)} %get-tuple-element.22), channel_id=1, source_target_pairs={{0,16},{8,24},{16,0},{24,8},{1,17},{9,25},{17,1},{25,9},{2,18},{10... | collective-permute-start | bytes 2128904 | tf_op jit(solution)/shard_map/ppermute | solution.py:23
  104.7 11.2 %collective-permute-start.10 = (f32[33,21,128]{2,0,1:T(8,128)S(1)}, f32[33,21,128]{2,0,1:T(8,128)S(1)}, u32[]{:S(2)}, u32[]{:S(2)}) collective-permute-start(f32[33,21,128]{2,0,1:T(8,128)S(1)} %slice_select_fusion.2), channel_id=1, source_target_pairs={{0,8},{8,0},{16,24},{24,16},{1,9},{9,1},{17,25},{25,17},{2,10},{10... | collective-permute-start | bytes 1064456 | tf_op jit(solution)/shard_map/ppermute | solution.py:23
  105.3 10.9 %collective-permute-start.9 = (f32[33,21,128]{2,0,1:T(8,128)S(1)}, f32[33,21,128]{2,0,1:T(8,128)S(1)}, u32[]{:S(2)}, u32[]{:S(2)}) collective-permute-start(f32[33,21,128]{2,0,1:T(8,128)S(1)} %slice_select_fusion.3), channel_id=1, source_target_pairs={{0,16},{8,24},{16,0},{24,8},{1,17},{9,25},{17,1},{25,9},{2,18},{10... | collective-permute-start | bytes 1064456 | tf_op jit(solution)/shard_map/ppermute | solution.py:23
  116.4 10.1 %collective-permute-start.11 = (f32[33,21,128]{2,0,1:T(8,128)S(1)}, f32[33,21,128]{2,0,1:T(8,128)S(1)}, u32[]{:S(2)}, u32[]{:S(2)}) collective-permute-start(f32[33,21,128]{2,0,1:T(8,128)S(1)} %select_add_fusion.3), channel_id=1, source_target_pairs={{0,16},{8,24},{16,0},{24,8},{1,17},{9,25},{17,1},{25,9},{2,18},{10... | collective-permute-start | bytes 1064456 | tf_op jit(solution)/shard_map/ppermute | solution.py:23
  118.0 9.7 %collective-permute-start.12 = (f32[33,21,128]{2,0,1:T(8,128)S(1)}, f32[33,21,128]{2,0,1:T(8,128)S(1)}, u32[]{:S(2)}, u32[]{:S(2)}) collective-permute-start(f32[33,21,128]{2,0,1:T(8,128)S(1)} %select_add_fusion.2), channel_id=1, source_target_pairs={{0,8},{8,0},{16,24},{24,16},{1,9},{9,1},{17,25},{25,17},{2,10},{10... | collective-permute-start | bytes 1064456 | tf_op jit(solution)/shard_map/ppermute | solution.py:23
  128.4 16.3 %collective-permute-start.13 = (f32[66,21,128]{2,0,1:T(8,128)S(1)}, f32[66,21,128]{2,0,1:T(8,128)S(1)}, u32[]{:S(2)}, u32[]{:S(2)}) collective-permute-start(f32[66,21,128]{2,0,1:T(8,128)S(1)} %copy.47), channel_id=1, source_target_pairs={{0,8},{8,0},{16,24},{24,16},{1,9},{9,1},{17,25},{25,17},{2,10},{10... | collective-permute-start | bytes 2128904 | tf_op jit(solution)/shard_map/ppermute | solution.py:23
  130.0 15.9 %collective-permute-start.14 = (f32[66,21,128]{2,0,1:T(8,128)S(1)}, f32[66,21,128]{2,0,1:T(8,128)S(1)}, u32[]{:S(2)}, u32[]{:S(2)}) collective-permute-start(f32[66,21,128]{2,0,1:T(8,128)S(1)} %copy.48), channel_id=1, source_target_pairs={{0,16},{8,24},{16,0},{24,8},{1,17},{9,25},{17,1},{25,9},{2,18},{10... | collective-permute-start | bytes 2128904 | tf_op jit(solution)/shard_map/ppermute | solution.py:23

commit v7 on v4

--- a/solution.py
+++ b/solution.py
@@ -128,27 +128,42 @@
         (((0,), (1,)), ((), ())),
         precision=lax.Precision.HIGHEST,
     )
-    cells = positions * slot_count
-    slot_rows = -(-slot_energy.size // cells)
-    energy_rows = -(-events // cells)
-    used = events * fold + slot_rows + energy_rows
-    spare = -used % (2 * sta_size)
-    flat_slot = jnp.pad(slot_energy.reshape(-1), (0, slot_rows * cells - slot_energy.size))
-    flat_event = jnp.pad(event_energy, (0, energy_rows * cells - events))
-    packed = jnp.concatenate(
-        [
-            lag_scores,
-            flat_slot.reshape(slot_rows, positions, slot_count),
-            flat_event.reshape(energy_rows, positions, slot_count),
-            jnp.zeros((spare, positions, slot_count), jnp.float32),
-        ],
-        axis=0,
-    )
-    total = sta_allreduce(packed)
+    waste = positions * fold - lag_count
+    room = events * waste * slot_count
+    needed = slot_energy.size + events
     base = events * fold
-    slot_all = total[base : base + slot_rows].reshape(-1)[: lag_count * slot_count]
-    event_all = total[base + slot_rows : base + slot_rows + energy_rows].reshape(-1)[:events]
-    scores_all = total[:base].reshape(events, fold, positions, slot_count)
+    if waste and room >= needed and base % (4 * sta_size) == 0:
+        stash = jnp.pad(
+            jnp.concatenate([slot_energy.reshape(-1), event_energy]), (0, room - needed)
+        ).reshape(events, waste, slot_count)
+        grid = lag_scores.reshape(events, fold, positions, slot_count)
+        grid = grid.at[:, fold - waste :, positions - 1, :].set(stash)
+        packed = with_layout_constraint(grid.reshape(base, positions, slot_count), Layout((1, 0, 2)))
+        total = sta_allreduce(packed).reshape(events, fold, positions, slot_count)
+        spilled = total[:, fold - waste :, positions - 1, :].reshape(-1)
+        slot_all = spilled[: slot_energy.size]
+        event_all = spilled[slot_energy.size : needed]
+        scores_all = total
+    else:
+        cells = positions * slot_count
+        slot_rows = -(-slot_energy.size // cells)
+        energy_rows = -(-events // cells)
+        spare = -(base + slot_rows + energy_rows) % (2 * sta_size)
+        flat_slot = jnp.pad(slot_energy.reshape(-1), (0, slot_rows * cells - slot_energy.size))
+        flat_event = jnp.pad(event_energy, (0, energy_rows * cells - events))
+        packed = jnp.concatenate(
+            [
+                lag_scores,
+                flat_slot.reshape(slot_rows, positions, slot_count),
+                flat_event.reshape(energy_rows, positions, slot_count),
+                jnp.zeros((spare, positions, slot_count), jnp.float32),
+            ],
+            axis=0,
+        )
+        total = sta_allreduce(packed)
+        slot_all = total[base : base + slot_rows].reshape(-1)[: slot_energy.size]
+        event_all = total[base + slot_rows : base + slot_rows + energy_rows].reshape(-1)[:events]
+        scores_all = total[:base].reshape(events, fold, positions, slot_count)
     scores_all = jnp.transpose(scores_all, (0, 2, 1, 3)).reshape(
         events, positions * fold, slot_count
     )[:, :lag_count]

time: 146 us -> 139 us (0.952)
  waiting for transfers between devices: 95.9 us -> 89.5 us
    ppermute x8, waiting for transfers between devices: 48.3 us -> 41.7 us  [exchange(): return lax.ppermute(value, axis, [(i, i ^ bit) for i in range(size)])]
where the time goes in v7:
time: 139 us; the launch traced here: 138 us
  waiting for transfers between devices  89.5 us (64%)
  local copies, waits for them, and re-layouts  15.9 us (11%)
  starting transfers between devices  15 us (11%)
  matrix products  10.3 us (7%)
  other arithmetic  7.28 us (5%)
    all_to_all x1, waiting for transfers between devices, body(): lax.all_to_all(outgoing, 'evt', split_axis=0, concat_axis=0, tiled=True)  47.7 us
    ppermute x8, waiting for transfers between devices, exchange(): return lax.ppermute(value, axis, [(i, i ^ bit) for i in range(size)])  41.7 us
    conv_general_dilated x1, matrix products, body(): lax.conv_general_dilated(widened, expanded, (fold,), 'VALID', dimension_n...  10 us
    ppermute x8, starting transfers between devices, exchange(): return lax.ppermute(value, axis, [(i, i ^ bit) for i in range(size)])  8.53 us
    all_to_all x1, starting transfers between devices, body(): lax.all_to_all(outgoing, 'evt', split_axis=0, concat_axis=0, tiled=True)  6.45 us
    all_to_all x1, local copies, waits for them, and re-layouts, body(): lax.all_to_all(outgoing, 'evt', split_axis=0, concat_axis=0, tiled=True)  4.54 us
    reshape x1, local copies, waits for them, and re-layouts, body(): expanded = jnp.stack(shifted, axis=1).reshape(events * fold, channels, span)  3.85 us
  transfers between devices with their start and end apart: 9, of which 8 were waited for; matrix products, arithmetic and copies ran while one was open for 5% of the time, Pallas kernels for 0%

profile of v7, /device:TPU:0, one launch (start us, length us, event | category | flops | bytes accessed | tf_op | source)
XLA Modules:
  0.0 138.2 jit_solution(15143521688814476628)
XLA Ops:
  0.0 0.8 copy.41
  0.8 0.1 reshape.152
  0.9 0.1 fusion.4
  1.0 0.2 reduce_window_sum.11
  1.2 0.2 select_reduce_fusion.1
  1.4 0.1 fusion.3
  1.5 0.1 select_reduce_fusion
  1.6 1.4 %pad.30 = bf16[65,24,280]{2,1,0:T(8,128)(2,1)S(1)} pad(bf16[64,24,280]{2,1,0:T(8,128)(2,1)} %param.5, bf16[]{:T(256)} %constant.66.clone.1), padding=0_1x0_0x0_0 | pad | bytes 1733762 | tf_op jit(solution)/shard_map/jit(_pad)/pad | solution.py:88
  3.0 2.3 %gather_fusion = bf16[128,24,280]{2,1,0:T(8,128)(2,1)} fusion(bf16[65,24,280]{2,1,0:T(8,128)(2,1)S(1)} %pad.30, s32[1024]{0:T(1024)S(1)} %pad_clamp_fusion), kind=kCustom, calls=%fused_computation | custom fusion | bytes 3441152 | tf_op jit(solution)/shard_map/jit(_take)/gather | solution.py:89
  5.3 0.0 copy-start.2
  5.3 0.0 copy-start.1
  5.3 6.5 %all-to-all-start = ((bf16[128,24,280]{2,1,0:T(8,128)(2,1)}), bf16[128,24,280]{2,1,0:T(8,128)(2,1)}, u32[]{:S(2)}, u32[]{:S(2)}) async-start(bf16[128,24,280]{2,1,0:T(8,128)(2,1)} %gather_fusion), calls=%async_computation | async-start | bytes 4718592 | tf_op jit(solution)/shard_map/all_to_all | solution.py:92
  11.8 0.0 copy-done.2
  11.8 0.0 copy-done.1
  11.8 1.0 multiply_reduce_fusion.1
  12.8 0.9 pad_bitcast_fusion.3
  13.7 0.8 pad_maximum_fusion
  14.6 0.4 copy.43
  15.0 3.8 %copy.44 = bf16[256,24,203]{0,1,2:T(8,128)(2,1)} copy(bf16[256,24,203]{2,1,0:T(8,128)(2,1)S(1)} %bitcast.36) | data formatting | bytes 4988928 | tf_op jit(solution)/shard_map/reshape | solution.py:109
  18.8 47.7 %all-to-all-done = bf16[128,24,280]{2,1,0:T(8,128)(2,1)} async-done(((bf16[128,24,280]{2,1,0:T(8,128)(2,1)}), bf16[128,24,280]{2,1,0:T(8,128)(2,1)}, u32[]{:S(2)}, u32[]{:S(2)}) %all-to-all-start) | async-done | bytes 1720352 | tf_op jit(solution)/shard_map/all_to_all | solution.py:92
  66.6 4.5 %copy.42 = bf16[128,24,280]{0,1,2:T(8,128)(2,1)} copy(bf16[128,24,280]{2,1,0:T(8,128)(2,1)} %all-to-all-done) | data formatting | bytes 3440640 | tf_op jit(solution)/shard_map/all_to_all | solution.py:92
  71.1 0.0 copy-start
  71.1 10.0 %fusion.6 = f32[256,21,128]{2,0,1:T(8,128)S(1)} fusion(bf16[128,24,280]{0,1,2:T(8,128)(2,1)} %copy.42, bf16[256,24,203]{0,1,2:T(8,128)(2,1)} %copy.44), kind=kOutput, calls=%fused_computation.45 | convolution fusion | flops 6700400640 | bytes 6967296 | tf_op jit(solution)/shard_map/conv_general_dilated | solution.py:111
  81.1 0.0 copy-done
  81.1 1.2 multiply_reduce_fusion
  82.3 0.3 convolution_bitcast_fusion
  82.7 0.6 scatter.4
  83.4 0.2 slice_select_fusion
  83.6 1.6 %collective-permute-start = (f32[64,21,128]{2,0,1:T(8,128)S(1)}, f32[64,21,128]{2,0,1:T(8,128)S(1)}, u32[]{:S(2)}, u32[]{:S(2)}) collective-permute-start(f32[64,21,128]{2,0,1:T(8,128)S(1)} %get-tuple-element.33), channel_id=1, source_target_pairs={{0,8},{8,0},{16,24},{24,16},{1,9},{9,1},{17,25},{25,17},{2,10},{10... | collective-permute-start | bytes 2064392 | tf_op jit(solution)/shard_map/ppermute | solution.py:23
  85.2 1.5 %collective-permute-start.1 = (f32[64,21,128]{2,0,1:T(8,128)S(1)}, f32[64,21,128]{2,0,1:T(8,128)S(1)}, u32[]{:S(2)}, u32[]{:S(2)}) collective-permute-start(f32[64,21,128]{2,0,1:T(8,128)S(1)} %get-tuple-element.34), channel_id=1, source_target_pairs={{0,16},{8,24},{16,0},{24,8},{1,17},{9,25},{17,1},{25,9},{2,18},{10... | collective-permute-start | bytes 2064392 | tf_op jit(solution)/shard_map/ppermute | solution.py:23
  86.7 14.0 %collective-permute-done = f32[64,21,128]{2,0,1:T(8,128)S(1)} collective-permute-done((f32[64,21,128]{2,0,1:T(8,128)S(1)}, f32[64,21,128]{2,0,1:T(8,128)S(1)}, u32[]{:S(2)}, u32[]{:S(2)}) %collective-permute-start) | collective-permute-done | bytes 688160 | tf_op jit(solution)/shard_map/ppermute | solution.py:23
  100.7 1.2 collective-permute-done.1
  101.9 0.4 select_add_fusion
  102.4 1.6 %collective-permute-start.2 = (f32[32,21,128]{2,0,1:T(8,128)S(1)}, f32[32,21,128]{2,0,1:T(8,128)S(1)}, u32[]{:S(2)}, u32[]{:S(2)}) collective-permute-start(f32[32,21,128]{2,0,1:T(8,128)S(1)} %slice_select_fusion.3), channel_id=1, source_target_pairs={{0,16},{8,24},{16,0},{24,8},{1,17},{9,25},{17,1},{25,9},{2,18},{10... | collective-permute-start | bytes 1032200 | tf_op jit(solution)/shard_map/ppermute | solution.py:23
  104.0 0.5 collective-permute-start.3
  104.5 6.3 %collective-permute-done.2 = f32[32,21,128]{2,0,1:T(8,128)S(1)} collective-permute-done((f32[32,21,128]{2,0,1:T(8,128)S(1)}, f32[32,21,128]{2,0,1:T(8,128)S(1)}, u32[]{:S(2)}, u32[]{:S(2)}) %collective-permute-start.2) | collective-permute-done | bytes 344096 | tf_op jit(solution)/shard_map/ppermute | solution.py:23
  110.8 1.2 collective-permute-done.3
  112.1 0.1 select_add_fusion.2
  112.2 0.1 select_add_fusion.3
  112.3 0.6 collective-permute-start.4
  112.9 0.6 collective-permute-start.5
  113.4 6.2 %collective-permute-done.4 = f32[32,21,128]{2,0,1:T(8,128)S(1)} collective-permute-done((f32[32,21,128]{2,0,1:T(8,128)S(1)}, f32[32,21,128]{2,0,1:T(8,128)S(1)}, u32[]{:S(2)}, u32[]{:S(2)}) %collective-permute-start.4) | collective-permute-done | bytes 344096 | tf_op jit(solution)/shard_map/ppermute | solution.py:23
  119.6 1.3 collective-permute-done.5
  121.0 0.1 maximum_select_fusion.3
  121.0 0.1 copy.46
  121.1 0.1 maximum_select_fusion.2
  121.2 0.1 copy.45
  121.2 0.6 collective-permute-start.6
  121.8 1.6 %collective-permute-start.7 = (f32[64,21,128]{2,0,1:T(8,128)S(1)}, f32[64,21,128]{2,0,1:T(8,128)S(1)}, u32[]{:S(2)}, u32[]{:S(2)}) collective-permute-start(f32[64,21,128]{2,0,1:T(8,128)S(1)} %bitcast.46), channel_id=1, source_target_pairs={{0,16},{8,24},{16,0},{24,8},{1,17},{9,25},{17,1},{25,9},{2,18},{10... | collective-permute-start | bytes 2064392 | tf_op jit(solution)/shard_map/ppermute | solution.py:23
  123.4 11.5 %collective-permute-done.6 = f32[64,21,128]{2,0,1:T(8,128)S(1)} collective-permute-done((f32[64,21,128]{2,0,1:T(8,128)S(1)}, f32[64,21,128]{2,0,1:T(8,128)S(1)}, u32[]{:S(2)}, u32[]{:S(2)}) %collective-permute-start.6) | collective-permute-done | bytes 688160 | tf_op jit(solution)/shard_map/ppermute | solution.py:23
  134.9 0.0 collective-permute-done.7
  134.9 0.2 maximum_select_fusion
  135.0 0.1 copy.47
  135.1 0.1 maximum_select_fusion.1
  135.3 0.1 copy.48
  135.4 0.3 pad_maximum_fusion.1
  135.8 0.4 copy.49
  136.2 0.1 reshape_squeeze.3
  136.3 1.9 %slice_multiply_fusion = f32[64,81,128]{2,0,1:T(8,128)} fusion(f32[64,84,128]{2,0,1:T(8,128)S(1)} %bitcast.43, f32[81,128]{1,0:T(8,128)S(1)} %mul.52, f32[64]{0:T(128)S(1)} %slice.119), kind=kLoop, calls=%fused_computation.4 | loop fusion | flops 1990656 | bytes 5350144 | tf_op jit(solution)/shard_map/div | solution.py:19
  (13 shorter events, 0.3 us)
Async XLA Ops:
  5.3 6.5 %copy-start.2 = (s32[24]{0:T(128)S(1)}, s32[24]{0:T(128)}, u32[]{:S(2)}) copy-start(s32[24]{0:T(128)} %param.6) | copy-start | bytes 292
  5.3 6.5 %copy-start.1 = (bf16[64,24,280]{2,1,0:T(8,128)(2,1)S(1)}, bf16[64,24,280]{2,1,0:T(8,128)(2,1)}, u32[]{:S(2)}) copy-start(bf16[64,24,280]{2,1,0:T(8,128)(2,1)} %param.5) | copy-start | bytes 2580484
  5.3 61.2 %all-to-all-start = ((bf16[128,24,280]{2,1,0:T(8,128)(2,1)}), bf16[128,24,280]{2,1,0:T(8,128)(2,1)}, u32[]{:S(2)}, u32[]{:S(2)}) async-start(bf16[128,24,280]{2,1,0:T(8,128)(2,1)} %gather_fusion), calls=%async_computation | async-start | bytes 4718592 | tf_op jit(solution)/shard_map/all_to_all | solution.py:92
  71.1 10.0 %copy-start = (bf16[128,24,280]{0,1,2:T(8,128)(2,1)S(1)}, bf16[128,24,280]{0,1,2:T(8,128)(2,1)}, u32[]{:S(2)}) copy-start(bf16[128,24,280]{0,1,2:T(8,128)(2,1)} %copy.42) | copy-start | bytes 5160964
  83.6 17.0 %collective-permute-start = (f32[64,21,128]{2,0,1:T(8,128)S(1)}, f32[64,21,128]{2,0,1:T(8,128)S(1)}, u32[]{:S(2)}, u32[]{:S(2)}) collective-permute-start(f32[64,21,128]{2,0,1:T(8,128)S(1)} %get-tuple-element.33), channel_id=1, source_target_pairs={{0,8},{8,0},{16,24},{24,16},{1,9},{9,1},{17,25},{25,17},{2,10},{10... | collective-permute-start | bytes 2064392 | tf_op jit(solution)/shard_map/ppermute | solution.py:23
  85.2 16.7 %collective-permute-start.1 = (f32[64,21,128]{2,0,1:T(8,128)S(1)}, f32[64,21,128]{2,0,1:T(8,128)S(1)}, u32[]{:S(2)}, u32[]{:S(2)}) collective-permute-start(f32[64,21,128]{2,0,1:T(8,128)S(1)} %get-tuple-element.34), channel_id=1, source_target_pairs={{0,16},{8,24},{16,0},{24,8},{1,17},{9,25},{17,1},{25,9},{2,18},{10... | collective-permute-start | bytes 2064392 | tf_op jit(solution)/shard_map/ppermute | solution.py:23
  102.4 8.5 %collective-permute-start.2 = (f32[32,21,128]{2,0,1:T(8,128)S(1)}, f32[32,21,128]{2,0,1:T(8,128)S(1)}, u32[]{:S(2)}, u32[]{:S(2)}) collective-permute-start(f32[32,21,128]{2,0,1:T(8,128)S(1)} %slice_select_fusion.3), channel_id=1, source_target_pairs={{0,16},{8,24},{16,0},{24,8},{1,17},{9,25},{17,1},{25,9},{2,18},{10... | collective-permute-start | bytes 1032200 | tf_op jit(solution)/shard_map/ppermute | solution.py:23
  104.0 8.1 %collective-permute-start.3 = (f32[32,21,128]{2,0,1:T(8,128)S(1)}, f32[32,21,128]{2,0,1:T(8,128)S(1)}, u32[]{:S(2)}, u32[]{:S(2)}) collective-permute-start(f32[32,21,128]{2,0,1:T(8,128)S(1)} %slice_select_fusion.2), channel_id=1, source_target_pairs={{0,8},{8,0},{16,24},{24,16},{1,9},{9,1},{17,25},{25,17},{2,10},{10... | collective-permute-start | bytes 1032200 | tf_op jit(solution)/shard_map/ppermute | solution.py:23
  112.3 7.3 %collective-permute-start.4 = (f32[32,21,128]{2,0,1:T(8,128)S(1)}, f32[32,21,128]{2,0,1:T(8,128)S(1)}, u32[]{:S(2)}, u32[]{:S(2)}) collective-permute-start(f32[32,21,128]{2,0,1:T(8,128)S(1)} %select_add_fusion.3), channel_id=1, source_target_pairs={{0,16},{8,24},{16,0},{24,8},{1,17},{9,25},{17,1},{25,9},{2,18},{10... | collective-permute-start | bytes 1032200 | tf_op jit(solution)/shard_map/ppermute | solution.py:23
  112.9 8.1 %collective-permute-start.5 = (f32[32,21,128]{2,0,1:T(8,128)S(1)}, f32[32,21,128]{2,0,1:T(8,128)S(1)}, u32[]{:S(2)}, u32[]{:S(2)}) collective-permute-start(f32[32,21,128]{2,0,1:T(8,128)S(1)} %select_add_fusion.2), channel_id=1, source_target_pairs={{0,8},{8,0},{16,24},{24,16},{1,9},{9,1},{17,25},{25,17},{2,10},{10... | collective-permute-start | bytes 1032200 | tf_op jit(solution)/shard_map/ppermute | solution.py:23
  121.2 13.6 %collective-permute-start.6 = (f32[64,21,128]{2,0,1:T(8,128)S(1)}, f32[64,21,128]{2,0,1:T(8,128)S(1)}, u32[]{:S(2)}, u32[]{:S(2)}) collective-permute-start(f32[64,21,128]{2,0,1:T(8,128)S(1)} %bitcast.48), channel_id=1, source_target_pairs={{0,8},{8,0},{16,24},{24,16},{1,9},{9,1},{17,25},{25,17},{2,10},{10... | collective-permute-start | bytes 2064392 | tf_op jit(solution)/shard_map/ppermute | solution.py:23
  121.8 13.0 %collective-permute-start.7 = (f32[64,21,128]{2,0,1:T(8,128)S(1)}, f32[64,21,128]{2,0,1:T(8,128)S(1)}, u32[]{:S(2)}, u32[]{:S(2)}) collective-permute-start(f32[64,21,128]{2,0,1:T(8,128)S(1)} %bitcast.46), channel_id=1, source_target_pairs={{0,16},{8,24},{16,0},{24,8},{1,17},{9,25},{17,1},{25,9},{2,18},{10... | collective-permute-start | bytes 2064392 | tf_op jit(solution)/shard_map/ppermute | solution.py:23
